TPU v7x, 256 devices: a whole 4x4x8 slice. The times are simulated.
256 devices in a mesh: patch: 32 (over x, y, z_hi), stream: 8 (over z_lo, core).
Axes of the slice: x: 4, y: 4, z: 8 (z_hi: 2, z_lo: 4; z = z_hi * 4 + z_lo), core: 2. Of those that a mesh axis runs over, the one named last changes fastest.
Arguments:
- exposures: bfloat16 [4, 8, 512, 8, 4096], P(None, 'stream', 'patch'), may hold values from -6 to 6
- owners: int32 [4, 8, 512, 2], P(None, 'stream', 'patch'), may hold values from 0 to 31, all different within a row; in each aligned block of 16 rows (0 to 15, 16 to 31, ..., all dimensions but the last counted through in order) at most 2 rows name the same one
- offsets: int32 [4, 8, 512, 2], P(None, 'stream', 'patch'), may hold values from 0 to 56
- visit_shift: float32 [4, 8, 2], P(None, 'stream'), may hold values from 0.05 to 0.95
- visit_weight: float32 [4, 8], P(None, 'stream'), may hold values from 0.25 to 4
- psf_class: int32 [4, 8], P(None, 'stream'), may hold values from 0 to 7
- coef_table: float32 [8, 16], replicated, may hold values from -0.18 to 0.18
- basis_x: float32 [16, 31], replicated, may hold values from -1 to 1
- basis_y: float32 [16, 31], replicated, may hold values from -1 to 1
Outputs:
- coadd: float32 [2048, 4096], P(('patch', 'stream'))
Inputs may be any that keep to these rules, and one draw needn't show every extreme that they name: `owners`: each row names 2 different patches; in each step the 16 strips of one holder name one patch at most 2 times, a bound that some block reaches.
All inputs are finite; a program needn't handle non-finite values.
Results may differ from a plain program's by a relative error of at most 0.0062.
Values may be sent and summed in bfloat16 or wider, within the bound.
No kernel may reach another device: no remote copies, remote signals or barrier semaphores. Data moves between devices by JAX's collectives and lax.ppermute only.
A program may use at most 128 MiB of HBM per device.

v0:
```python
import jax
import jax.numpy as jnp
from jax import lax
from jax.sharding import PartitionSpec as P

CAP = 2
SLAB_ROWS = 64


def lanczos_taps(fraction):
    distance = jnp.arange(6, dtype=jnp.int32).astype(jnp.float32) - 2.0 - fraction
    values = jnp.sinc(distance) * jnp.sinc(distance / 3.0)
    return values / jnp.sum(values)


def combined_taps(basis_rows, warp_x):
    summed = jnp.zeros((basis_rows.shape[0], basis_rows.shape[1] + 5), jnp.float32)
    for tap_slot in range(6):
        summed = summed + jnp.pad(basis_rows * warp_x[tap_slot], ((0, 0), (tap_slot, 5 - tap_slot)))
    return summed


def row_filter(slab_image, tap_values):
    row_count = slab_image.shape[0]
    width = slab_image.shape[1]
    blocks = width // 128
    padded = jnp.pad(slab_image, ((0, 0), (32, 96)))
    front_part = padded[:, :width].reshape(row_count, blocks, 128)
    second = padded[:, 128 : width + 128].reshape(row_count, blocks, 128)[:, :, :64]
    windows = jnp.concatenate([front_part, second], axis=2)
    band_index = (
        jnp.arange(192, dtype=jnp.int32)[:, None] - jnp.arange(128, dtype=jnp.int32)[None, :] - 15
    )
    selector = (
        band_index[:, :, None] == jnp.arange(tap_values.shape[1], dtype=jnp.int32)[None, None, :]
    ).astype(jnp.float32)
    band_matrix = jnp.einsum(
        "aom,bm->bao", selector, tap_values.astype(jnp.float32), precision=lax.Precision.HIGHEST
    )
    band_matrix = band_matrix.astype(jnp.bfloat16)
    filtered = jnp.einsum("rna,bao->brno", windows, band_matrix, preferred_element_type=jnp.float32)
    return filtered.astype(jnp.bfloat16).reshape(tap_values.shape[0] * row_count, width)


def mixing(weight, coeffs, basis_y, row_count):
    tap_index = (
        jnp.arange(row_count, dtype=jnp.int32)[None, :]
        - jnp.arange(row_count, dtype=jnp.int32)[:, None]
        + 15
    )
    selector = (
        tap_index[:, :, None] == jnp.arange(basis_y.shape[1], dtype=jnp.int32)[None, None, :]
    ).astype(jnp.float32)
    kernel_table = jnp.einsum("rsj,bj->rbs", selector, basis_y, precision=lax.Precision.HIGHEST)
    kernel_table = kernel_table * (weight * coeffs)[None, :, None]
    return kernel_table.astype(jnp.bfloat16).reshape(row_count, -1)


def pack(strips, owner_table, offset_table, patches):
    strip_count = strips.shape[0]
    fanout = owner_table.shape[1]
    target = owner_table.reshape(-1)
    target_hits = (target[:, None] == jnp.arange(patches, dtype=jnp.int32)[None, :]).astype(
        jnp.int32
    )
    earlier = jnp.cumsum(target_hits, axis=0) - target_hits
    position = jnp.sum(earlier * target_hits, axis=1)
    slot_index = target * CAP + position
    matches = (slot_index[None, :] == jnp.arange(patches * CAP, dtype=jnp.int32)[:, None]).astype(
        jnp.int32
    )
    strip_select = jnp.sum(matches.reshape(patches * CAP, strip_count, fanout), axis=2).astype(
        jnp.bfloat16
    )
    outgoing = jnp.dot(
        strip_select, strips.reshape(strip_count, -1), preferred_element_type=jnp.bfloat16
    )
    filled = jnp.sum(matches, axis=1)
    slot_offset = jnp.sum(matches * offset_table.reshape(-1)[None, :], axis=1) + (filled - 1) * (
        SLAB_ROWS + 8
    )
    return (
        outgoing.reshape(patches, CAP, strips.shape[1], strips.shape[2]),
        slot_offset.reshape(patches, CAP),
    )


def place(received, recv_off, warp_y):
    strip_rows = received.shape[-2]
    width = received.shape[-1]
    starts = recv_off.reshape(-1)
    local_row = jnp.arange(SLAB_ROWS, dtype=jnp.int32)[:, None] - starts[None, :]
    inside = (local_row >= 0) & (local_row < strip_rows)
    tap_index = jnp.arange(strip_rows, dtype=jnp.int32)[None, None, :] - local_row[:, :, None] + 2
    tap_hits = (tap_index[:, :, :, None] == jnp.arange(6, dtype=jnp.int32)).astype(jnp.float32)
    tap_values = jnp.sum(tap_hits * warp_y, axis=3)
    tap_values = (
        jnp.where(inside[:, :, None], tap_values, 0.0).astype(jnp.bfloat16).reshape(SLAB_ROWS, -1)
    )
    return jnp.dot(tap_values, received.reshape(-1, width), preferred_element_type=jnp.float32)


def visit_term(received, recv_off, shifts, weight, psf_index, coef_table, basis_x, basis_y):
    warp_x = lanczos_taps(shifts[0])
    warp_y = lanczos_taps(shifts[1])
    slab_image = place(received, recv_off, warp_y).astype(jnp.bfloat16)
    tap_values = combined_taps(basis_x, warp_x).astype(jnp.bfloat16)
    filtered = row_filter(slab_image, tap_values)
    class_hits = (psf_index == jnp.arange(coef_table.shape[0], dtype=jnp.int32)).astype(jnp.float32)
    coeffs = jnp.sum(class_hits[:, None] * coef_table, axis=0)
    mix_matrix = mixing(weight, coeffs, basis_y, SLAB_ROWS)
    return jnp.dot(mix_matrix, filtered, preferred_element_type=jnp.float32)


def shards(
    exposures, owners, offsets, visit_shift, visit_weight, psf_class, coef_table, basis_x, basis_y
):
    patches = lax.axis_size("patch")
    step_count = exposures.shape[0]
    width = exposures.shape[4]
    partial_sum = jnp.zeros((SLAB_ROWS, width), jnp.float32)
    for step_index in range(step_count):
        outgoing, slot_offset = pack(
            exposures[step_index, 0], owners[step_index, 0], offsets[step_index, 0], patches
        )
        received, recv_off = (
            lax.all_to_all(outgoing, "patch", split_axis=0, concat_axis=0, tiled=True),
            lax.all_to_all(slot_offset, "patch", split_axis=0, concat_axis=0, tiled=True),
        )
        visit_part = visit_term(
            received,
            recv_off,
            visit_shift[step_index, 0],
            visit_weight[step_index, 0],
            psf_class[step_index, 0],
            coef_table,
            basis_x,
            basis_y,
        )
        partial_sum = partial_sum + visit_part
    stream_share = lax.psum_scatter(partial_sum, "stream", scatter_dimension=0, tiled=True)
    return stream_share


def solution(mesh):
    placed = (
        P(None, "stream", "patch", None, None),
        P(None, "stream", "patch", None),
        P(None, "stream", "patch", None),
        P(None, "stream", None),
        P(None, "stream"),
        P(None, "stream"),
        P(),
        P(),
        P(),
    )
    return jax.shard_map(
        shards, mesh=mesh, in_specs=placed, out_specs=P(("patch", "stream"), None), check_vma=False
    )
```

profile of v0, /device:TPU:8, one launch (start us, length us, event | category | flops | bytes accessed | tf_op | source)
XLA Modules:
  0.0 651.8 jit_solution(8615494811792976531)
XLA Ops:
  9.5 14.2 %all-to-all-start.6 = ((s32[32,1,2]{2,1,0:T(1,128)}), s32[32,1,2]{2,1,0:T(1,128)S(1)}, u32[]{:S(2)}, u32[]{:S(2)}) async-start(s32[32,1,2]{2,1,0:T(1,128)} %bitcast.82), calls=%async_computation.6 | async-start | bytes 32768 | tf_op jit(solution)/shard_map/all_to_all | solution.py:128
  34.5 8.6 %all-to-all-start.4 = ((s32[32,1,2]{2,1,0:T(1,128)}), s32[32,1,2]{2,1,0:T(1,128)S(1)}, u32[]{:S(2)}, u32[]{:S(2)}) async-start(s32[32,1,2]{2,1,0:T(1,128)} %bitcast.59), calls=%async_computation.4 | async-start | bytes 32768 | tf_op jit(solution)/shard_map/all_to_all | solution.py:128
  43.9 10.2 %all-to-all-done.4 = s32[32,1,2]{2,1,0:T(1,128)S(1)} async-done(((s32[32,1,2]{2,1,0:T(1,128)}), s32[32,1,2]{2,1,0:T(1,128)S(1)}, u32[]{:S(2)}, u32[]{:S(2)}) %all-to-all-start.4) | async-done | bytes 288 | tf_op jit(solution)/shard_map/all_to_all | solution.py:128
  59.8 10.1 %all-to-all-done.2 = s32[32,1,2]{2,1,0:T(1,128)S(1)} async-done(((s32[32,1,2]{2,1,0:T(1,128)}), s32[32,1,2]{2,1,0:T(1,128)S(1)}, u32[]{:S(2)}, u32[]{:S(2)}) %all-to-all-start.2) | async-done | bytes 288 | tf_op jit(solution)/shard_map/all_to_all | solution.py:128
  69.9 5.0 all-to-all-start
  85.9 9.0 %all-to-all-start.7 = ((bf16[32,2,8,4096]{3,2,1,0:T(8,128)(2,1)}), bf16[32,2,8,4096]{3,2,1,0:T(8,128)(2,1)}, u32[]{:S(2)}, u32[]{:S(2)}) async-start(bf16[32,2,8,4096]{3,2,1,0:T(8,128)(2,1)} %copy.177), calls=%async_computation.7 | async-start | bytes 8388608 | tf_op jit(solution)/shard_map/all_to_all | solution.py:127
  100.8 90.3 %all-to-all-done.7 = bf16[32,2,8,4096]{3,2,1,0:T(8,128)(2,1)} async-done(((bf16[32,2,8,4096]{3,2,1,0:T(8,128)(2,1)}), bf16[32,2,8,4096]{3,2,1,0:T(8,128)(2,1)}, u32[]{:S(2)}, u32[]{:S(2)}) %all-to-all-start.7) | async-done | bytes 4194336 | tf_op jit(solution)/shard_map/all_to_all | solution.py:127
  191.1 11.0 %all-to-all-start.5 = ((bf16[32,2,8,4096]{3,2,1,0:T(8,128)(2,1)}), bf16[32,2,8,4096]{3,2,1,0:T(8,128)(2,1)}, u32[]{:S(2)}, u32[]{:S(2)}) async-start(bf16[32,2,8,4096]{3,2,1,0:T(8,128)(2,1)} %copy.164), calls=%async_computation.5 | async-start | bytes 8388608 | tf_op jit(solution)/shard_map/all_to_all | solution.py:127
  208.1 89.3 %all-to-all-done.5 = bf16[32,2,8,4096]{3,2,1,0:T(8,128)(2,1)} async-done(((bf16[32,2,8,4096]{3,2,1,0:T(8,128)(2,1)}), bf16[32,2,8,4096]{3,2,1,0:T(8,128)(2,1)}, u32[]{:S(2)}, u32[]{:S(2)}) %all-to-all-start.5) | async-done | bytes 4194336 | tf_op jit(solution)/shard_map/all_to_all | solution.py:127
  297.5 11.1 %all-to-all-start.3 = ((bf16[32,2,8,4096]{3,2,1,0:T(8,128)(2,1)}), bf16[32,2,8,4096]{3,2,1,0:T(8,128)(2,1)}, u32[]{:S(2)}, u32[]{:S(2)}) async-start(bf16[32,2,8,4096]{3,2,1,0:T(8,128)(2,1)} %copy.151), calls=%async_computation.3 | async-start | bytes 8388608 | tf_op jit(solution)/shard_map/all_to_all | solution.py:127
  344.2 51.9 %all-to-all-done.3 = bf16[32,2,8,4096]{3,2,1,0:T(8,128)(2,1)} async-done(((bf16[32,2,8,4096]{3,2,1,0:T(8,128)(2,1)}), bf16[32,2,8,4096]{3,2,1,0:T(8,128)(2,1)}, u32[]{:S(2)}, u32[]{:S(2)}) %all-to-all-start.3) | async-done | bytes 4194336 | tf_op jit(solution)/shard_map/all_to_all | solution.py:127
  396.1 16.3 %all-to-all-start.1 = ((bf16[32,2,8,4096]{3,2,1,0:T(8,128)(2,1)}), bf16[32,2,8,4096]{3,2,1,0:T(8,128)(2,1)}, u32[]{:S(2)}, u32[]{:S(2)}) async-start(bf16[32,2,8,4096]{3,2,1,0:T(8,128)(2,1)} %copy.138), calls=%async_computation.1 | async-start | bytes 8388608 | tf_op jit(solution)/shard_map/all_to_all | solution.py:127
  420.3 11.1 %broadcast_multiply_fusion.23 = (f32[16,31]{1,0:T(8,128)S(1)}, f32[16,31]{1,0:T(8,128)S(1)}, f32[16,31]{1,0:T(8,128)S(1)}, f32[16,31]{1,0:T(8,128)S(1)}, f32[16,...) fusion(f32[16,31]{1,0:T(8,128)S(1)} %copy-done.7, ...), kind=kLoop, calls=%fused_computation.192 | loop fusion | flops 8928 | bytes 37768 | tf_op jit(solution)/shard_map/mul | solution.py:19
  448.7 5.5 convert_bitcast_fusion
  454.3 14.1 %copy.181 = bf16[16,64,32,128]{3,2,1,0:T(8,128)(2,1)} copy(bf16[16,64,32,128]{3,1,2,0:T(8,128)(2,1)} %convert_bitcast_fusion) | data formatting | bytes 16777216 | tf_op jit(solution)/shard_map/convert_element_type | solution.py:42
  472.2 5.6 convert_bitcast_fusion.1
  477.8 13.8 %copy.168 = bf16[16,64,32,128]{3,2,1,0:T(8,128)(2,1)} copy(bf16[16,64,32,128]{3,1,2,0:T(8,128)(2,1)} %convert_bitcast_fusion.1) | data formatting | bytes 16777216 | tf_op jit(solution)/shard_map/convert_element_type | solution.py:42
  495.4 5.5 convert_bitcast_fusion.2
  501.0 14.0 %copy.155 = bf16[16,64,32,128]{3,2,1,0:T(8,128)(2,1)} copy(bf16[16,64,32,128]{3,1,2,0:T(8,128)(2,1)} %convert_bitcast_fusion.2) | data formatting | bytes 16777216 | tf_op jit(solution)/shard_map/convert_element_type | solution.py:42
  518.9 5.5 convert_bitcast_fusion.3
  524.4 13.9 %copy.142 = bf16[16,64,32,128]{3,2,1,0:T(8,128)(2,1)} copy(bf16[16,64,32,128]{3,1,2,0:T(8,128)(2,1)} %convert_bitcast_fusion.3) | data formatting | bytes 16777216 | tf_op jit(solution)/shard_map/convert_element_type | solution.py:42
  538.3 6.2 fusion
  544.6 6.2 fusion.3
  557.6 87.2 %reduce-scatter.2.cloned.1.call-done = f32[8,4096]{1,0:T(8,128)} async-done(((f32[64,4096]{1,0:T(8,128)}), f32[8,4096]{1,0:T(8,128)}) %reduce-scatter.2.cloned.1.call-update) | async-done | bytes 131088 | tf_op jit(solution)/shard_map/reduce_scatter | solution.py:141
  (213 shorter events, 121.6 us)
Async XLA Ops:
  6.5 337.0 %copy-start = (f32[16,31]{1,0:T(8,128)S(1)}, f32[16,31]{1,0:T(8,128)}, u32[]{:S(2)}) copy-start(f32[16,31]{1,0:T(8,128)} %param.18) | copy-start | bytes 5956
  9.5 25.0 %all-to-all-start.6 = ((s32[32,1,2]{2,1,0:T(1,128)}), s32[32,1,2]{2,1,0:T(1,128)S(1)}, u32[]{:S(2)}, u32[]{:S(2)}) async-start(s32[32,1,2]{2,1,0:T(1,128)} %bitcast.82), calls=%async_computation.6 | async-start | bytes 32768 | tf_op jit(solution)/shard_map/all_to_all | solution.py:128
  34.5 19.6 %all-to-all-start.4 = ((s32[32,1,2]{2,1,0:T(1,128)}), s32[32,1,2]{2,1,0:T(1,128)S(1)}, u32[]{:S(2)}, u32[]{:S(2)}) async-start(s32[32,1,2]{2,1,0:T(1,128)} %bitcast.59), calls=%async_computation.4 | async-start | bytes 32768 | tf_op jit(solution)/shard_map/all_to_all | solution.py:128
  54.1 15.8 %all-to-all-start.2 = ((s32[32,1,2]{2,1,0:T(1,128)}), s32[32,1,2]{2,1,0:T(1,128)S(1)}, u32[]{:S(2)}, u32[]{:S(2)}) async-start(s32[32,1,2]{2,1,0:T(1,128)} %bitcast.36), calls=%async_computation.2 | async-start | bytes 32768 | tf_op jit(solution)/shard_map/all_to_all | solution.py:128
  69.9 16.0 %all-to-all-start = ((s32[32,1,2]{2,1,0:T(1,128)}), s32[32,1,2]{2,1,0:T(1,128)S(1)}, u32[]{:S(2)}, u32[]{:S(2)}) async-start(s32[32,1,2]{2,1,0:T(1,128)} %bitcast.13), calls=%async_computation | async-start | bytes 32768 | tf_op jit(solution)/shard_map/all_to_all | solution.py:128
  85.9 9.0 %copy-start.6 = (s32[32,1,2]{2,1,0:T(1,128)}, s32[32,1,2]{2,1,0:T(1,128)S(1)}, u32[]{:S(2)}) copy-start(s32[32,1,2]{2,1,0:T(1,128)S(1)} %all-to-all-done) | copy-start | bytes 772
  85.9 105.3 %all-to-all-start.7 = ((bf16[32,2,8,4096]{3,2,1,0:T(8,128)(2,1)}), bf16[32,2,8,4096]{3,2,1,0:T(8,128)(2,1)}, u32[]{:S(2)}, u32[]{:S(2)}) async-start(bf16[32,2,8,4096]{3,2,1,0:T(8,128)(2,1)} %copy.177), calls=%async_computation.7 | async-start | bytes 8388608 | tf_op jit(solution)/shard_map/all_to_all | solution.py:127
  191.1 106.3 %all-to-all-start.5 = ((bf16[32,2,8,4096]{3,2,1,0:T(8,128)(2,1)}), bf16[32,2,8,4096]{3,2,1,0:T(8,128)(2,1)}, u32[]{:S(2)}, u32[]{:S(2)}) async-start(bf16[32,2,8,4096]{3,2,1,0:T(8,128)(2,1)} %copy.164), calls=%async_computation.5 | async-start | bytes 8388608 | tf_op jit(solution)/shard_map/all_to_all | solution.py:127
  297.5 98.7 %all-to-all-start.3 = ((bf16[32,2,8,4096]{3,2,1,0:T(8,128)(2,1)}), bf16[32,2,8,4096]{3,2,1,0:T(8,128)(2,1)}, u32[]{:S(2)}, u32[]{:S(2)}) async-start(bf16[32,2,8,4096]{3,2,1,0:T(8,128)(2,1)} %copy.151), calls=%async_computation.3 | async-start | bytes 8388608 | tf_op jit(solution)/shard_map/all_to_all | solution.py:127
  310.2 4.4 copy-start.9
  310.2 15.2 %copy-start.10 = (s32[4,1]{0,1:T(1,128)S(1)}, s32[4,1]{0,1:T(1,128)}, u32[]{:S(2)}) copy-start(s32[4,1]{0,1:T(1,128)} %param.15) | copy-start | bytes 52
  310.2 27.2 %copy-start.11 = (f32[4,1]{0,1:T(1,128)S(1)}, f32[4,1]{0,1:T(1,128)}, u32[]{:S(2)}) copy-start(f32[4,1]{0,1:T(1,128)} %param.14) | copy-start | bytes 52
  310.3 30.6 %copy-start.12 = (f32[8,16]{1,0:T(8,128)S(1)}, f32[8,16]{1,0:T(8,128)}, u32[]{:S(2)}) copy-start(f32[8,16]{1,0:T(8,128)} %param.16) | copy-start | bytes 1540
  344.2 72.5 %copy-start.7 = (f32[16,31]{1,0:T(8,128)S(1)}, f32[16,31]{1,0:T(8,128)}, u32[]{:S(2)}) copy-start(f32[16,31]{1,0:T(8,128)} %param.17) | copy-start | bytes 5956
  396.1 118.9 %all-to-all-start.1 = ((bf16[32,2,8,4096]{3,2,1,0:T(8,128)(2,1)}), bf16[32,2,8,4096]{3,2,1,0:T(8,128)(2,1)}, u32[]{:S(2)}, u32[]{:S(2)}) async-start(bf16[32,2,8,4096]{3,2,1,0:T(8,128)(2,1)} %copy.138), calls=%async_computation.1 | async-start | bytes 8388608 | tf_op jit(solution)/shard_map/all_to_all | solution.py:127
  412.4 232.4 %reduce-scatter.2.cloned.1.call-start = ((), (), s32[]{:S(2)}) async-start(), calls=%async_computation.9 | async-start | bytes 1179648 | tf_op jit(solution)/shard_map/reduce_scatter | solution.py:141
  454.3 14.1 %copy-start.2 = (bf16[64,64,8]{0,2,1:T(8,128)(2,1)S(1)}, bf16[64,64,8]{0,2,1:T(8,128)(2,1)}, u32[]{:S(2)}) copy-start(bf16[64,64,8]{0,2,1:T(8,128)(2,1)} %copy.159) | copy-start | bytes 196612
  524.4 14.0 %copy-start.5 = (bf16[64,1024]{1,0:T(8,128)(2,1)S(1)}, bf16[64,1024]{1,0:T(8,128)(2,1)}, u32[]{:S(2)}) copy-start(bf16[64,1024]{1,0:T(8,128)(2,1)} %reshape.661) | copy-start | bytes 393220
  524.4 26.5 %slice-start.2 = ((s8[8388608]{0:T(1024)(128)(4,1)}), s8[4194304]{0:T(1024)(128)(4,1)S(1)}, s32[]{:S(2)}) async-start(s8[8388608]{0:T(1024)(128)(4,1)} %bitcast.284), calls=%async_computation.12 | async-start | bytes 8388608
  538.3 6.2 copy-start.4
  538.3 12.5 %slice-start.3 = ((s8[8388608]{0:T(1024)(128)(4,1)}), s8[4194304]{0:T(1024)(128)(4,1)S(1)}, s32[]{:S(2)}) async-start(s8[8388608]{0:T(1024)(128)(4,1)} %bitcast.284), calls=%async_computation.13 | async-start | bytes 8388608
  544.6 6.3 copy-start.3
  544.6 9.1 %slice-start = ((s8[8388608]{0:T(1024)(128)(4,1)}), s8[4194304]{0:T(1024)(128)(4,1)S(1)}, s32[]{:S(2)}) async-start(s8[8388608]{0:T(1024)(128)(4,1)} %bitcast.279), calls=%async_computation.10 | async-start | bytes 8388608
  553.7 91.2 %copy-start.1 = (f32[16,31]{1,0:T(8,128)S(1)}, f32[16,31]{1,0:T(8,128)}, u32[]{:S(2)}) copy-start(f32[16,31]{1,0:T(8,128)} %param.18) | copy-start | bytes 5956
  (2 other events, 7.1 us)
Sparse Core Ops, SparseCore 0:
  557.7 87.0 reduce-scatter.1
where the time goes:
time: 659 us; the launch traced here: 652 us
  waiting for transfers between devices  347 us (53%)
  local copies, waits for them, and re-layouts  97.6 us (15%)
  starting transfers between devices  80.2 us (12%)
  matrix products  64.9 us (10%)
  other arithmetic  48 us (7%)
  between operations  14.4 us (2%)
    all_to_all x4, waiting for transfers between devices, shards(): lax.all_to_all(outgoing, 'patch', split_axis=0, concat_axis=0, tiled=True)  232 us
    reduce_scatter x1, waiting for transfers between devices, shards(): lax.psum_scatter(partial_sum, 'stream', scatter_dimension=0, tiled=True)  87.2 us
    convert_element_type x4, local copies, waits for them, and re-layouts, row_filter(): filtered.astype(jnp.bfloat16)  55.8 us
    all_to_all x4, starting transfers between devices, shards(): lax.all_to_all(outgoing, 'patch', split_axis=0, concat_axis=0, tiled=True)  47.4 us
    all_to_all x4, starting transfers between devices, shards(): lax.all_to_all(slot_offset, 'patch', split_axis=0, concat_axis=0, tiled=T...  32.5 us
    all_to_all x4, waiting for transfers between devices, shards(): lax.all_to_all(slot_offset, 'patch', split_axis=0, concat_axis=0, tiled=T...  27.9 us
    dot_general x4, matrix products, row_filter(): jnp.einsum('rna,bao->brno', windows, band_matrix, preferred_element_type=...  22.2 us
    dot_general x4, matrix products, visit_term(): return jnp.dot(mix_matrix, filtered, preferred_element_type=jnp.float32)  19.1 us
  transfers between devices with their start and end apart: 9, of which 8 were waited for; matrix products, arithmetic and copies ran while one was open for 25% of the time, Pallas kernels for 0%

commit v1 on v0

--- a/solution.py
+++ b/solution.py
@@ -20,6 +20,12 @@
     return summed
 
 
+def toeplitz(period, count):
+    length = period.shape[-1] - 1
+    tiled = jnp.tile(period, [1] * (period.ndim - 1) + [count])
+    return tiled[..., : count * length].reshape(period.shape[:-1] + (count, length))
+
+
 def row_filter(slab_image, tap_values):
     row_count = slab_image.shape[0]
     width = slab_image.shape[1]
@@ -28,32 +34,19 @@
     front_part = padded[:, :width].reshape(row_count, blocks, 128)
     second = padded[:, 128 : width + 128].reshape(row_count, blocks, 128)[:, :, :64]
     windows = jnp.concatenate([front_part, second], axis=2)
-    band_index = (
-        jnp.arange(192, dtype=jnp.int32)[:, None] - jnp.arange(128, dtype=jnp.int32)[None, :] - 15
-    )
-    selector = (
-        band_index[:, :, None] == jnp.arange(tap_values.shape[1], dtype=jnp.int32)[None, None, :]
-    ).astype(jnp.float32)
-    band_matrix = jnp.einsum(
-        "aom,bm->bao", selector, tap_values.astype(jnp.float32), precision=lax.Precision.HIGHEST
-    )
-    band_matrix = band_matrix.astype(jnp.bfloat16)
-    filtered = jnp.einsum("rna,bao->brno", windows, band_matrix, preferred_element_type=jnp.float32)
+    taps = tap_values.shape[1]
+    band_rows = jnp.pad(tap_values, ((0, 0), (15, 193 - 15 - taps)))
+    band_matrix = toeplitz(band_rows, 128)
+    filtered = jnp.einsum("rna,boa->brno", windows, band_matrix, preferred_element_type=jnp.float32)
     return filtered.astype(jnp.bfloat16).reshape(tap_values.shape[0] * row_count, width)
 
 
 def mixing(weight, coeffs, basis_y, row_count):
-    tap_index = (
-        jnp.arange(row_count, dtype=jnp.int32)[None, :]
-        - jnp.arange(row_count, dtype=jnp.int32)[:, None]
-        + 15
-    )
-    selector = (
-        tap_index[:, :, None] == jnp.arange(basis_y.shape[1], dtype=jnp.int32)[None, None, :]
-    ).astype(jnp.float32)
-    kernel_table = jnp.einsum("rsj,bj->rbs", selector, basis_y, precision=lax.Precision.HIGHEST)
-    kernel_table = kernel_table * (weight * coeffs)[None, :, None]
-    return kernel_table.astype(jnp.bfloat16).reshape(row_count, -1)
+    reach = basis_y.shape[1] // 2
+    period = jnp.pad(basis_y, ((0, 0), (0, row_count + reach + 1 - basis_y.shape[1])))
+    kernel_table = toeplitz(period, row_count)[:, :, reach:]
+    kernel_table = kernel_table * (weight * coeffs)[:, None, None]
+    return kernel_table.astype(jnp.bfloat16).transpose(1, 0, 2).reshape(row_count, -1)
 
 
 def pack(strips, owner_table, offset_table, patches):
@@ -116,20 +109,23 @@
     exposures, owners, offsets, visit_shift, visit_weight, psf_class, coef_table, basis_x, basis_y
 ):
     patches = lax.axis_size("patch")
+    streams = lax.axis_size("stream")
     step_count = exposures.shape[0]
     width = exposures.shape[4]
+    packed = [
+        pack(exposures[step_index, 0], owners[step_index, 0], offsets[step_index, 0], patches)
+        for step_index in range(step_count)
+    ]
+    slot_offsets = jnp.stack([slot_offset for _, slot_offset in packed], axis=1)
+    recv_offsets = lax.all_to_all(slot_offsets, "patch", split_axis=0, concat_axis=0, tiled=True)
     partial_sum = jnp.zeros((SLAB_ROWS, width), jnp.float32)
     for step_index in range(step_count):
-        outgoing, slot_offset = pack(
-            exposures[step_index, 0], owners[step_index, 0], offsets[step_index, 0], patches
-        )
-        received, recv_off = (
-            lax.all_to_all(outgoing, "patch", split_axis=0, concat_axis=0, tiled=True),
-            lax.all_to_all(slot_offset, "patch", split_axis=0, concat_axis=0, tiled=True),
+        received = lax.all_to_all(
+            packed[step_index][0], "patch", split_axis=0, concat_axis=0, tiled=True
         )
         visit_part = visit_term(
             received,
-            recv_off,
+            recv_offsets[:, step_index],
             visit_shift[step_index, 0],
             visit_weight[step_index, 0],
             psf_class[step_index, 0],
@@ -138,8 +134,12 @@
             basis_y,
         )
         partial_sum = partial_sum + visit_part
-    stream_share = lax.psum_scatter(partial_sum, "stream", scatter_dimension=0, tiled=True)
-    return stream_share
+    share_rows = SLAB_ROWS // streams
+    pieces = lax.all_to_all(
+        partial_sum.reshape(streams, share_rows, width), "stream", split_axis=0, concat_axis=0,
+        tiled=True,
+    )
+    return jnp.sum(pieces, axis=0)
 
 
 def solution(mesh):

time: 659 us -> 562 us (0.85)
  waiting for transfers between devices: 347 us -> 239 us
  blocking collectives: 0 us -> 29 us
  local copies, waits for them, and re-layouts: 97.6 us -> 115 us
  starting transfers between devices: 80.2 us -> 63.7 us
  between operations: 14.4 us -> 1.15 us
  matrix products: 64.9 us -> 56.2 us
    reduce_scatter x1 -> x0, waiting for transfers between devices: 87.2 us -> none  [shards(): lax.psum_scatter(partial_sum, 'stream', scatter_dimension=0, tiled=True)]
    all_to_all x0 -> x1, blocking collectives: none -> 29 us  [shards(): lax.all_to_all(partial_sum.reshape(streams, share_rows, width), 'stream',...]
    all_to_all x8 -> x5, waiting for transfers between devices: 259 us -> 239 us  [the longest x4 237 us: shards(): lax.all_to_all(packed[step_index][0], 'patch', split_axis=0, concat_axis=...]
    all_to_all x8 -> x5, starting transfers between devices: 79.9 us -> 63.7 us  [the longest x4 49.6 us: shards(): lax.all_to_all(packed[step_index][0], 'patch', split_axis=0, concat_axis=...]
    reshape x4 -> x9, local copies, waits for them, and re-layouts: 2.75 us -> 10.5 us  [the longest x5 7.73 us: toeplitz(): tiled[..., :count * length].reshape(period.shape[:-1] + (count, length))]
    another operation x0 -> x11, local copies, waits for them, and re-layouts: none -> 7.11 us  [the longest x10 6.2 us: toeplitz(): tiled = jnp.tile(period, [1] * (period.ndim - 1) + [count])]
    dot_general x9 -> x4, matrix products: 26.2 us -> 19.4 us  [row_filter(): jnp.einsum('rna,boa->brno', windows, band_matrix, preferred_element_type=...]
  transfers between devices with their start and end apart: 9 -> 5, of which waited for: 8 -> 4; matrix products, arithmetic and copies ran while one was open for 25% -> 31% of each run, Pallas kernels for 0% -> 0%
where the time goes in v1:
time: 562 us; the launch traced here: 553 us
  waiting for transfers between devices  239 us (43%)
  local copies, waits for them, and re-layouts  115 us (20%)
  starting transfers between devices  63.7 us (11%)
  matrix products  56.2 us (10%)
  other arithmetic  49.4 us (9%)
  blocking collectives  29 us (5%)
    all_to_all x4, waiting for transfers between devices, shards(): lax.all_to_all(packed[step_index][0], 'patch', split_axis=0, concat_axis=...  237 us
    convert_element_type x4, local copies, waits for them, and re-layouts, row_filter(): filtered.astype(jnp.bfloat16)  54.7 us
    all_to_all x4, starting transfers between devices, shards(): lax.all_to_all(packed[step_index][0], 'patch', split_axis=0, concat_axis=...  49.6 us
    all_to_all x1, blocking collectives, shards(): lax.all_to_all(partial_sum.reshape(streams, share_rows, width), 'stream',...  29 us
    dot_general x4, matrix products, row_filter(): jnp.einsum('rna,boa->brno', windows, band_matrix, preferred_element_type=...  19.4 us
    dot_general x4, matrix products, visit_term(): return jnp.dot(mix_matrix, filtered, preferred_element_type=jnp.float32)  18.3 us
    dot_general x4, local copies, waits for them, and re-layouts, pack(): jnp.dot(strip_select, strips.reshape(strip_count, -1), preferred_element_...  17.1 us
    mul x2, other arithmetic, combined_taps(): basis_rows * warp_x[tap_slot]  15 us
  transfers between devices with their start and end apart: 5, of which 4 were waited for; matrix products, arithmetic and copies ran while one was open for 31% of the time, Pallas kernels for 0%

profile of v1, /device:TPU:8, one launch (start us, length us, event | category | flops | bytes accessed | tf_op | source)
XLA Modules:
  0.0 552.6 jit_solution(11291630272075606917)
XLA Ops:
  6.0 14.2 %all-to-all-start = ((s32[32,4,2]{1,2,0:T(2,128)}), s32[32,4,2]{1,2,0:T(2,128)S(1)}, u32[]{:S(2)}, u32[]{:S(2)}) async-start(s32[32,4,2]{1,2,0:T(2,128)} %copy.200), calls=%async_computation | async-start | bytes 65536 | tf_op jit(solution)/shard_map/all_to_all | solution.py:120
  25.8 4.2 copy.239
  31.1 11.2 %all-to-all-start.4 = ((bf16[32,2,8,4096]{3,2,1,0:T(8,128)(2,1)}), bf16[32,2,8,4096]{3,2,1,0:T(8,128)(2,1)}, u32[]{:S(2)}, u32[]{:S(2)}) async-start(bf16[32,2,8,4096]{3,2,1,0:T(8,128)(2,1)} %copy.239), calls=%async_computation.4 | async-start | bytes 8388608 | tf_op jit(solution)/shard_map/all_to_all | solution.py:123
  43.9 4.3 copy.228
  48.2 93.4 %all-to-all-done.4 = bf16[32,2,8,4096]{3,2,1,0:T(8,128)(2,1)} async-done(((bf16[32,2,8,4096]{3,2,1,0:T(8,128)(2,1)}), bf16[32,2,8,4096]{3,2,1,0:T(8,128)(2,1)}, u32[]{:S(2)}, u32[]{:S(2)}) %all-to-all-start.4) | async-done | bytes 4194336 | tf_op jit(solution)/shard_map/all_to_all | solution.py:123
  141.6 10.3 %all-to-all-start.3 = ((bf16[32,2,8,4096]{3,2,1,0:T(8,128)(2,1)}), bf16[32,2,8,4096]{3,2,1,0:T(8,128)(2,1)}, u32[]{:S(2)}, u32[]{:S(2)}) async-start(bf16[32,2,8,4096]{3,2,1,0:T(8,128)(2,1)} %copy.228), calls=%async_computation.3 | async-start | bytes 8388608 | tf_op jit(solution)/shard_map/all_to_all | solution.py:123
  153.7 4.2 copy.217
  157.9 90.2 %all-to-all-done.3 = bf16[32,2,8,4096]{3,2,1,0:T(8,128)(2,1)} async-done(((bf16[32,2,8,4096]{3,2,1,0:T(8,128)(2,1)}), bf16[32,2,8,4096]{3,2,1,0:T(8,128)(2,1)}, u32[]{:S(2)}, u32[]{:S(2)}) %all-to-all-start.3) | async-done | bytes 4194336 | tf_op jit(solution)/shard_map/all_to_all | solution.py:123
  248.1 13.0 %all-to-all-start.2 = ((bf16[32,2,8,4096]{3,2,1,0:T(8,128)(2,1)}), bf16[32,2,8,4096]{3,2,1,0:T(8,128)(2,1)}, u32[]{:S(2)}, u32[]{:S(2)}) async-start(bf16[32,2,8,4096]{3,2,1,0:T(8,128)(2,1)} %copy.217), calls=%async_computation.2 | async-start | bytes 8388608 | tf_op jit(solution)/shard_map/all_to_all | solution.py:123
  272.6 4.3 copy.206
  290.6 11.3 %broadcast_multiply_fusion.23 = (f32[16,31]{1,0:T(8,128)S(1)}, f32[16,31]{1,0:T(8,128)S(1)}, f32[16,31]{1,0:T(8,128)S(1)}, f32[16,31]{1,0:T(8,128)S(1)}, f32[16,...) fusion(f32[16,31]{1,0:T(8,128)S(1)} %copy-done.5, ...), kind=kLoop, calls=%fused_computation.171 | loop fusion | flops 8928 | bytes 37768 | tf_op jit(solution)/shard_map/mul | solution.py:19
  301.9 53.9 %all-to-all-done.2 = bf16[32,2,8,4096]{3,2,1,0:T(8,128)(2,1)} async-done(((bf16[32,2,8,4096]{3,2,1,0:T(8,128)(2,1)}), bf16[32,2,8,4096]{3,2,1,0:T(8,128)(2,1)}, u32[]{:S(2)}, u32[]{:S(2)}) %all-to-all-start.2) | async-done | bytes 4194336 | tf_op jit(solution)/shard_map/all_to_all | solution.py:123
  355.8 15.0 %all-to-all-start.1 = ((bf16[32,2,8,4096]{3,2,1,0:T(8,128)(2,1)}), bf16[32,2,8,4096]{3,2,1,0:T(8,128)(2,1)}, u32[]{:S(2)}, u32[]{:S(2)}) async-start(bf16[32,2,8,4096]{3,2,1,0:T(8,128)(2,1)} %copy.206), calls=%async_computation.1 | async-start | bytes 8388608 | tf_op jit(solution)/shard_map/all_to_all | solution.py:123
  418.4 4.6 convert_bitcast_fusion
  423.0 13.7 %copy.243 = bf16[16,64,32,128]{3,2,1,0:T(8,128)(2,1)} copy(bf16[16,64,32,128]{3,1,2,0:T(8,128)(2,1)} %convert_bitcast_fusion) | data formatting | bytes 16777216 | tf_op jit(solution)/shard_map/convert_element_type | solution.py:41
  440.7 4.9 convert_bitcast_fusion.1
  445.5 13.6 %copy.232 = bf16[16,64,32,128]{3,2,1,0:T(8,128)(2,1)} copy(bf16[16,64,32,128]{3,1,2,0:T(8,128)(2,1)} %convert_bitcast_fusion.1) | data formatting | bytes 16777216 | tf_op jit(solution)/shard_map/convert_element_type | solution.py:41
  463.0 5.0 convert_bitcast_fusion.2
  468.1 13.6 %copy.221 = bf16[16,64,32,128]{3,2,1,0:T(8,128)(2,1)} copy(bf16[16,64,32,128]{3,1,2,0:T(8,128)(2,1)} %convert_bitcast_fusion.2) | data formatting | bytes 16777216 | tf_op jit(solution)/shard_map/convert_element_type | solution.py:41
  485.6 4.8 convert_bitcast_fusion.3
  490.4 13.8 %copy.210 = bf16[16,64,32,128]{3,2,1,0:T(8,128)(2,1)} copy(bf16[16,64,32,128]{3,1,2,0:T(8,128)(2,1)} %convert_bitcast_fusion.3) | data formatting | bytes 16777216 | tf_op jit(solution)/shard_map/convert_element_type | solution.py:41
  504.2 6.2 %fusion = f32[64,4096]{1,0:T(8,128)S(1)} fusion(bf16[64,1024]{1,0:T(8,128)(2,1)S(1)} %copy-done.2, bf16[128,8,32,128]{3,2,1,0:T(8,128)(2,1)} %bitcast.278), kind=kOutput, calls=%fused_computation | convolution fusion | flops 536870912 | bytes 9568256 | tf_op jit(solution)/shard_map/dot_general | solution.py:105
  510.5 6.5 %fusion.3 = f32[64,4096]{1,0:T(8,128)S(1)} fusion(bf16[64,1024]{1,0:T(8,128)(2,1)S(1)} %copy-done.3, bf16[128,8,32,128]{3,2,1,0:T(8,128)(2,1)} %bitcast.279), kind=kOutput, calls=%fused_computation.3 | convolution fusion | flops 536870912 | bytes 9568256 | tf_op jit(solution)/shard_map/dot_general | solution.py:105
  522.6 29.0 %all_to_all.30 = f32[8,8,4096]{2,1,0:T(8,128)S(1)} all-to-all(f32[8,8,4096]{2,1,0:T(8,128)S(1)} %fusion.21), channel_id=1, replica_groups=mesh['patch'=32,'stream'=8] {'stream'}, dimensions={0} | all-to-all | bytes 2097152 | tf_op jit(solution)/shard_map/all_to_all | solution.py:138
  (226 shorter events, 106.1 us)
Async XLA Ops:
  6.0 25.1 %all-to-all-start = ((s32[32,4,2]{1,2,0:T(2,128)}), s32[32,4,2]{1,2,0:T(2,128)S(1)}, u32[]{:S(2)}, u32[]{:S(2)}) async-start(s32[32,4,2]{1,2,0:T(2,128)} %copy.200), calls=%async_computation | async-start | bytes 65536 | tf_op jit(solution)/shard_map/all_to_all | solution.py:120
  31.1 110.5 %all-to-all-start.4 = ((bf16[32,2,8,4096]{3,2,1,0:T(8,128)(2,1)}), bf16[32,2,8,4096]{3,2,1,0:T(8,128)(2,1)}, u32[]{:S(2)}, u32[]{:S(2)}) async-start(bf16[32,2,8,4096]{3,2,1,0:T(8,128)(2,1)} %copy.239), calls=%async_computation.4 | async-start | bytes 8388608 | tf_op jit(solution)/shard_map/all_to_all | solution.py:123
  141.6 106.5 %all-to-all-start.3 = ((bf16[32,2,8,4096]{3,2,1,0:T(8,128)(2,1)}), bf16[32,2,8,4096]{3,2,1,0:T(8,128)(2,1)}, u32[]{:S(2)}, u32[]{:S(2)}) async-start(bf16[32,2,8,4096]{3,2,1,0:T(8,128)(2,1)} %copy.228), calls=%async_computation.3 | async-start | bytes 8388608 | tf_op jit(solution)/shard_map/all_to_all | solution.py:123
  157.9 103.2 %copy-start.7 = (f32[16,31]{1,0:T(8,128)S(1)}, f32[16,31]{1,0:T(8,128)}, u32[]{:S(2)}) copy-start(f32[16,31]{1,0:T(8,128)} %param.18) | copy-start | bytes 5956
  157.9 104.4 %copy-start.8 = (s32[4,1]{0,1:T(1,128)S(1)}, s32[4,1]{0,1:T(1,128)}, u32[]{:S(2)}) copy-start(s32[4,1]{0,1:T(1,128)} %param.15) | copy-start | bytes 52
  157.9 107.6 %copy-start.9 = (f32[4,1]{0,1:T(1,128)S(1)}, f32[4,1]{0,1:T(1,128)}, u32[]{:S(2)}) copy-start(f32[4,1]{0,1:T(1,128)} %param.14) | copy-start | bytes 52
  157.9 108.3 %copy-start.11 = (f32[8,16]{1,0:T(8,128)S(1)}, f32[8,16]{1,0:T(8,128)}, u32[]{:S(2)}) copy-start(f32[8,16]{1,0:T(8,128)} %param.16) | copy-start | bytes 1540
  248.1 107.7 %all-to-all-start.2 = ((bf16[32,2,8,4096]{3,2,1,0:T(8,128)(2,1)}), bf16[32,2,8,4096]{3,2,1,0:T(8,128)(2,1)}, u32[]{:S(2)}, u32[]{:S(2)}) async-start(bf16[32,2,8,4096]{3,2,1,0:T(8,128)(2,1)} %copy.217), calls=%async_computation.2 | async-start | bytes 8388608 | tf_op jit(solution)/shard_map/all_to_all | solution.py:123
  272.6 4.4 copy-start.6
  272.6 18.0 %copy-start.5 = (f32[16,31]{1,0:T(8,128)S(1)}, f32[16,31]{1,0:T(8,128)}, u32[]{:S(2)}) copy-start(f32[16,31]{1,0:T(8,128)} %param.17) | copy-start | bytes 5956
  355.8 125.9 %all-to-all-start.1 = ((bf16[32,2,8,4096]{3,2,1,0:T(8,128)(2,1)}), bf16[32,2,8,4096]{3,2,1,0:T(8,128)(2,1)}, u32[]{:S(2)}, u32[]{:S(2)}) async-start(bf16[32,2,8,4096]{3,2,1,0:T(8,128)(2,1)} %copy.206), calls=%async_computation.1 | async-start | bytes 8388608 | tf_op jit(solution)/shard_map/all_to_all | solution.py:123
  410.4 0.6 copy-start.10
  423.0 13.7 %copy-start.1 = (bf16[64,64,8]{0,2,1:T(8,128)(2,1)S(1)}, bf16[64,64,8]{0,2,1:T(8,128)(2,1)}, u32[]{:S(2)}) copy-start(bf16[64,64,8]{0,2,1:T(8,128)(2,1)} %copy.223) | copy-start | bytes 196612
  436.7 4.0 copy-start
  490.4 13.8 %copy-start.2 = (bf16[64,1024]{1,0:T(8,128)(2,1)S(1)}, bf16[64,1024]{1,0:T(8,128)(2,1)}, u32[]{:S(2)}) copy-start(bf16[64,1024]{1,0:T(8,128)(2,1)} %reshape.656) | copy-start | bytes 393220
  490.4 26.5 %slice-start.2 = ((s8[8388608]{0:T(1024)(128)(4,1)}), s8[4194304]{0:T(1024)(128)(4,1)S(1)}, s32[]{:S(2)}) async-start(s8[8388608]{0:T(1024)(128)(4,1)} %bitcast.280), calls=%async_computation.8 | async-start | bytes 8388608
  504.2 6.3 %copy-start.3 = (bf16[64,1024]{1,0:T(8,128)(2,1)S(1)}, bf16[64,1024]{1,0:T(8,128)(2,1)}, u32[]{:S(2)}) copy-start(bf16[64,1024]{1,0:T(8,128)(2,1)} %reshape.650) | copy-start | bytes 393220
  504.2 12.7 %slice-start.3 = ((s8[8388608]{0:T(1024)(128)(4,1)}), s8[4194304]{0:T(1024)(128)(4,1)S(1)}, s32[]{:S(2)}) async-start(s8[8388608]{0:T(1024)(128)(4,1)} %bitcast.280), calls=%async_computation.9 | async-start | bytes 8388608
  510.5 6.5 %copy-start.4 = (bf16[64,1024]{1,0:T(8,128)(2,1)S(1)}, bf16[64,1024]{1,0:T(8,128)(2,1)}, u32[]{:S(2)}) copy-start(bf16[64,1024]{1,0:T(8,128)(2,1)} %reshape.644) | copy-start | bytes 393220
  510.5 9.3 %slice-start = ((s8[8388608]{0:T(1024)(128)(4,1)}), s8[4194304]{0:T(1024)(128)(4,1)S(1)}, s32[]{:S(2)}) async-start(s8[8388608]{0:T(1024)(128)(4,1)} %bitcast.275), calls=%async_computation.6 | async-start | bytes 8388608
  517.0 2.8 slice-start.1

commit v2 on v1

--- a/solution.py
+++ b/solution.py
@@ -118,13 +118,16 @@
     ]
     slot_offsets = jnp.stack([slot_offset for _, slot_offset in packed], axis=1)
     recv_offsets = lax.all_to_all(slot_offsets, "patch", split_axis=0, concat_axis=0, tiled=True)
+    outgoing = [strips_out for strips_out, _ in packed]
+    received = [None] * step_count
+    for step_index in range(min(2, step_count)):
+        received[step_index] = lax.all_to_all(
+            outgoing[step_index], "patch", split_axis=0, concat_axis=0, tiled=True
+        )
     partial_sum = jnp.zeros((SLAB_ROWS, width), jnp.float32)
     for step_index in range(step_count):
-        received = lax.all_to_all(
-            packed[step_index][0], "patch", split_axis=0, concat_axis=0, tiled=True
-        )
         visit_part = visit_term(
-            received,
+            received[step_index],
             recv_offsets[:, step_index],
             visit_shift[step_index, 0],
             visit_weight[step_index, 0],
@@ -134,6 +137,12 @@
             basis_y,
         )
         partial_sum = partial_sum + visit_part
+        later = step_index + 2
+        if later < step_count:
+            released, partial_sum = lax.optimization_barrier((outgoing[later], partial_sum))
+            received[later] = lax.all_to_all(
+                released, "patch", split_axis=0, concat_axis=0, tiled=True
+            )
     share_rows = SLAB_ROWS // streams
     pieces = lax.all_to_all(
         partial_sum.reshape(streams, share_rows, width), "stream", split_axis=0, concat_axis=0,

time: 562 us -> 588 us (1.046)
  matrix products: 56.2 us -> 73.1 us
    optimization_barrier x0 -> x2, local copies, waits for them, and re-layouts: none -> 10.8 us  [shards(): lax.optimization_barrier((outgoing[later], partial_sum))]
    dot_general x4, matrix products: 19.4 us -> 28.1 us  [row_filter(): jnp.einsum('rna,boa->brno', windows, band_matrix, preferred_element_type=...]
    dot_general x4 -> x2, local copies, waits for them, and re-layouts: 17.1 us -> 8.49 us  [pack(): jnp.dot(strip_select, strips.reshape(strip_count, -1), preferred_element_...]
  transfers between devices with their start and end apart: 5 -> 5, of which waited for: 4 -> 4; matrix products, arithmetic and copies ran while one was open for 31% -> 30% of each run, Pallas kernels for 0% -> 0%
where the time goes in v2:
time: 588 us; the launch traced here: 578 us
  waiting for transfers between devices  237 us (40%)
  local copies, waits for them, and re-layouts  119 us (20%)
  matrix products  73.1 us (12%)
  starting transfers between devices  61.7 us (10%)
  other arithmetic  52 us (9%)
  blocking collectives  34.2 us (6%)
    all_to_all x2, waiting for transfers between devices, shards(): lax.all_to_all(released, 'patch', split_axis=0, concat_axis=0, tiled=True)  143 us
    all_to_all x2, waiting for transfers between devices, shards(): lax.all_to_all(outgoing[step_index], 'patch', split_axis=0, concat_axis=0...  93.4 us
    convert_element_type x4, local copies, waits for them, and re-layouts, row_filter(): filtered.astype(jnp.bfloat16)  54.6 us
    all_to_all x1, blocking collectives, shards(): lax.all_to_all(partial_sum.reshape(streams, share_rows, width), 'stream',...  34.2 us
    dot_general x4, matrix products, row_filter(): jnp.einsum('rna,boa->brno', windows, band_matrix, preferred_element_type=...  28.1 us
    all_to_all x2, starting transfers between devices, shards(): lax.all_to_all(released, 'patch', split_axis=0, concat_axis=0, tiled=True)  25.7 us
    all_to_all x2, starting transfers between devices, shards(): lax.all_to_all(outgoing[step_index], 'patch', split_axis=0, concat_axis=0...  21.8 us
    dot_general x4, matrix products, visit_term(): return jnp.dot(mix_matrix, filtered, preferred_element_type=jnp.float32)  21.5 us
  transfers between devices with their start and end apart: 5, of which 4 were waited for; matrix products, arithmetic and copies ran while one was open for 30% of the time, Pallas kernels for 0%

profile of v2, /device:TPU:8, one launch (start us, length us, event | category | flops | bytes accessed | tf_op | source)
XLA Modules:
  0.0 578.4 jit_solution(6477892224290372969)
XLA Ops:
  6.0 14.2 %all-to-all-start = ((s32[32,4,2]{1,2,0:T(2,128)}), s32[32,4,2]{1,2,0:T(2,128)S(1)}, u32[]{:S(2)}, u32[]{:S(2)}) async-start(s32[32,4,2]{1,2,0:T(2,128)} %copy.208), calls=%async_computation | async-start | bytes 65536 | tf_op jit(solution)/shard_map/all_to_all | solution.py:120
  31.1 11.6 %all-to-all-start.1 = ((bf16[32,2,8,4096]{3,2,1,0:T(8,128)(2,1)}), bf16[32,2,8,4096]{3,2,1,0:T(8,128)(2,1)}, u32[]{:S(2)}, u32[]{:S(2)}) async-start(bf16[32,2,8,4096]{3,2,1,0:T(8,128)(2,1)} %copy.214), calls=%async_computation.1 | async-start | bytes 8388608 | tf_op jit(solution)/shard_map/all_to_all | solution.py:124
  48.6 93.4 %all-to-all-done.1 = bf16[32,2,8,4096]{3,2,1,0:T(8,128)(2,1)} async-done(((bf16[32,2,8,4096]{3,2,1,0:T(8,128)(2,1)}), bf16[32,2,8,4096]{3,2,1,0:T(8,128)(2,1)}, u32[]{:S(2)}, u32[]{:S(2)}) %all-to-all-start.1) | async-done | bytes 4194336 | tf_op jit(solution)/shard_map/all_to_all | solution.py:124
  142.0 10.2 %all-to-all-start.2 = ((bf16[32,2,8,4096]{3,2,1,0:T(8,128)(2,1)}), bf16[32,2,8,4096]{3,2,1,0:T(8,128)(2,1)}, u32[]{:S(2)}, u32[]{:S(2)}) async-start(bf16[32,2,8,4096]{3,2,1,0:T(8,128)(2,1)} %copy.225), calls=%async_computation.2 | async-start | bytes 8388608 | tf_op jit(solution)/shard_map/all_to_all | solution.py:124
  180.5 11.8 %broadcast_multiply_fusion.11 = (f32[16,31]{1,0:T(8,128)S(1)}, f32[16,31]{1,0:T(8,128)S(1)}, f32[16,31]{1,0:T(8,128)S(1)}, f32[16,31]{1,0:T(8,128)S(1)}, f32[16,...) fusion(f32[16,31]{1,0:T(8,128)S(1)} %copy-done.6, ...), kind=kLoop, calls=%fused_computation.157 | loop fusion | flops 8928 | bytes 37768 | tf_op jit(solution)/shard_map/mul | solution.py:19
  210.0 4.7 fusion.30
  227.0 13.4 %convert_bitcast_fusion.3 = bf16[16,64,32,128]{3,1,2,0:T(8,128)(2,1)} fusion(bf16[64,32,64]{2,0,1:T(8,128)(2,1)S(1)} %copy.268, bf16[64,32,128]{2,0,1:T(8,128)(2,1)S(1)} %bitcast.283, bf16[16,128,192]{2,1,0:T(8,128)(2,1)S(1)} %reshape.639), kind=kOutput, calls=%fused_computation.15 | convolution fusion | flops 1616379904 | bytes 9961472 | tf_op jit(solution)/shard_map/rna,boa->brno/dot_general | solution.py:40
  240.5 13.7 %copy.218 = bf16[16,64,32,128]{3,2,1,0:T(8,128)(2,1)} copy(bf16[16,64,32,128]{3,1,2,0:T(8,128)(2,1)} %convert_bitcast_fusion.3) | data formatting | bytes 16777216 | tf_op jit(solution)/shard_map/convert_element_type | solution.py:41
  254.1 6.1 %fusion.9 = f32[64,4096]{1,0:T(8,128)S(1)} fusion(bf16[64,1024]{1,0:T(8,128)(2,1)S(1)} %copy-done.4, bf16[128,8,32,128]{3,2,1,0:T(8,128)(2,1)} %bitcast.278), kind=kOutput, calls=%fused_computation.9 | convolution fusion | flops 536870912 | bytes 9568256 | tf_op jit(solution)/shard_map/dot_general | solution.py:105
  264.1 5.0 convert_bitcast_fusion.2
  269.1 13.7 %copy.229 = bf16[16,64,32,128]{3,2,1,0:T(8,128)(2,1)} copy(bf16[16,64,32,128]{3,1,2,0:T(8,128)(2,1)} %convert_bitcast_fusion.2) | data formatting | bytes 16777216 | tf_op jit(solution)/shard_map/convert_element_type | solution.py:41
  282.7 6.3 %fusion.12 = f32[64,4096]{1,0:T(8,128)S(1)} fusion(f32[64,4096]{1,0:T(8,128)S(1)} %fusion.9, bf16[64,1024]{1,0:T(8,128)(2,1)S(1)} %copy-done.3, bf16[128,8,32,128]{3,2,1,0:T(8,128)(2,1)} %bitcast.276), kind=kOutput, calls=%fused_computation.16 | convolution fusion | flops 537133056 | bytes 10616832 | tf_op jit(solution)/shard_map/dot_general | solution.py:105
  289.0 4.4 copy.239
  293.5 12.2 %all-to-all-start.4 = ((bf16[32,2,8,4096]{3,2,1,0:T(8,128)(2,1)}), bf16[32,2,8,4096]{3,2,1,0:T(8,128)(2,1)}, u32[]{:S(2)}, u32[]{:S(2)}) async-start(bf16[32,2,8,4096]{3,2,1,0:T(8,128)(2,1)} %copy.239), calls=%async_computation.4 | async-start | bytes 8388608 | tf_op jit(solution)/shard_map/all_to_all | solution.py:143
  305.7 6.4 %copy.232 = bf16[32,2,8,4096]{3,2,1,0:T(8,128)(2,1)} copy(bf16[32,2,8,4096]{3,0,2,1:T(8,128)(2,1)} %fusion.28) | data formatting | bytes 8388608 | tf_op jit(solution)/shard_map/optimization_barrier | solution.py:142
  312.2 89.3 %all-to-all-done.4 = bf16[32,2,8,4096]{3,2,1,0:T(8,128)(2,1)} async-done(((bf16[32,2,8,4096]{3,2,1,0:T(8,128)(2,1)}), bf16[32,2,8,4096]{3,2,1,0:T(8,128)(2,1)}, u32[]{:S(2)}, u32[]{:S(2)}) %all-to-all-start.4) | async-done | bytes 4194336 | tf_op jit(solution)/shard_map/all_to_all | solution.py:143
  401.5 13.5 %all-to-all-start.3 = ((bf16[32,2,8,4096]{3,2,1,0:T(8,128)(2,1)}), bf16[32,2,8,4096]{3,2,1,0:T(8,128)(2,1)}, u32[]{:S(2)}, u32[]{:S(2)}) async-start(bf16[32,2,8,4096]{3,2,1,0:T(8,128)(2,1)} %copy.232), calls=%async_computation.3 | async-start | bytes 8388608 | tf_op jit(solution)/shard_map/all_to_all | solution.py:143
  439.7 4.8 convert_bitcast_fusion
  444.5 13.6 %copy.243 = bf16[16,64,32,128]{3,2,1,0:T(8,128)(2,1)} copy(bf16[16,64,32,128]{3,1,2,0:T(8,128)(2,1)} %convert_bitcast_fusion) | data formatting | bytes 16777216 | tf_op jit(solution)/shard_map/convert_element_type | solution.py:41
  458.2 53.3 %all-to-all-done.3 = bf16[32,2,8,4096]{3,2,1,0:T(8,128)(2,1)} async-done(((bf16[32,2,8,4096]{3,2,1,0:T(8,128)(2,1)}), bf16[32,2,8,4096]{3,2,1,0:T(8,128)(2,1)}, u32[]{:S(2)}, u32[]{:S(2)}) %all-to-all-start.3) | async-done | bytes 4194336 | tf_op jit(solution)/shard_map/all_to_all | solution.py:143
  515.3 4.9 convert_bitcast_fusion.1
  520.3 13.7 %copy.236 = bf16[16,64,32,128]{3,2,1,0:T(8,128)(2,1)} copy(bf16[16,64,32,128]{3,1,2,0:T(8,128)(2,1)} %convert_bitcast_fusion.1) | data formatting | bytes 16777216 | tf_op jit(solution)/shard_map/convert_element_type | solution.py:41
  533.9 6.3 %fusion = f32[64,4096]{1,0:T(8,128)S(1)} fusion(bf16[64,1024]{1,0:T(8,128)(2,1)S(1)} %copy-done.5, bf16[128,8,32,128]{3,2,1,0:T(8,128)(2,1)} %bitcast.277), kind=kOutput, calls=%fused_computation | convolution fusion | flops 536870912 | bytes 9568256 | tf_op jit(solution)/shard_map/dot_general | solution.py:105
  543.1 34.2 %all_to_all.30 = f32[8,8,4096]{2,1,0:T(8,128)S(1)} all-to-all(f32[8,8,4096]{2,1,0:T(8,128)S(1)} %fusion.21), channel_id=1, replica_groups=mesh['patch'=32,'stream'=8] {'stream'}, dimensions={0} | all-to-all | bytes 2097152 | tf_op jit(solution)/shard_map/all_to_all | solution.py:147
  (232 shorter events, 116.5 us)
Async XLA Ops:
  6.0 25.1 %all-to-all-start = ((s32[32,4,2]{1,2,0:T(2,128)}), s32[32,4,2]{1,2,0:T(2,128)S(1)}, u32[]{:S(2)}, u32[]{:S(2)}) async-start(s32[32,4,2]{1,2,0:T(2,128)} %copy.208), calls=%async_computation | async-start | bytes 65536 | tf_op jit(solution)/shard_map/all_to_all | solution.py:120
  20.8 3.6 copy-start.13
  31.1 110.9 %all-to-all-start.1 = ((bf16[32,2,8,4096]{3,2,1,0:T(8,128)(2,1)}), bf16[32,2,8,4096]{3,2,1,0:T(8,128)(2,1)}, u32[]{:S(2)}, u32[]{:S(2)}) async-start(bf16[32,2,8,4096]{3,2,1,0:T(8,128)(2,1)} %copy.214), calls=%async_computation.1 | async-start | bytes 8388608 | tf_op jit(solution)/shard_map/all_to_all | solution.py:124
  48.6 103.7 %copy-start.15 = (f32[16,31]{1,0:T(8,128)S(1)}, f32[16,31]{1,0:T(8,128)}, u32[]{:S(2)}) copy-start(f32[16,31]{1,0:T(8,128)} %param.18) | copy-start | bytes 5956
  48.6 105.1 %copy-start.16 = (s32[4,1]{0,1:T(1,128)S(1)}, s32[4,1]{0,1:T(1,128)}, u32[]{:S(2)}) copy-start(s32[4,1]{0,1:T(1,128)} %param.15) | copy-start | bytes 52
  48.6 108.4 %copy-start.17 = (f32[4,1]{0,1:T(1,128)S(1)}, f32[4,1]{0,1:T(1,128)}, u32[]{:S(2)}) copy-start(f32[4,1]{0,1:T(1,128)} %param.14) | copy-start | bytes 52
  48.6 109.1 %copy-start.19 = (f32[8,16]{1,0:T(8,128)S(1)}, f32[8,16]{1,0:T(8,128)}, u32[]{:S(2)}) copy-start(f32[8,16]{1,0:T(8,128)} %param.16) | copy-start | bytes 1540
  142.0 118.2 %all-to-all-start.2 = ((bf16[32,2,8,4096]{3,2,1,0:T(8,128)(2,1)}), bf16[32,2,8,4096]{3,2,1,0:T(8,128)(2,1)}, u32[]{:S(2)}, u32[]{:S(2)}) async-start(bf16[32,2,8,4096]{3,2,1,0:T(8,128)(2,1)} %copy.225), calls=%async_computation.2 | async-start | bytes 8388608 | tf_op jit(solution)/shard_map/all_to_all | solution.py:124
  152.2 10.4 %copy-start.14 = (f32[4,1,2]{0,2,1:T(2,128)S(1)}, f32[4,1,2]{0,2,1:T(2,128)}, u32[]{:S(2)}) copy-start(f32[4,1,2]{0,2,1:T(2,128)} %param.13) | copy-start | bytes 100
  152.3 23.9 %copy-start.6 = (f32[16,31]{1,0:T(8,128)S(1)}, f32[16,31]{1,0:T(8,128)}, u32[]{:S(2)}) copy-start(f32[16,31]{1,0:T(8,128)} %param.17) | copy-start | bytes 5956
  240.4 13.7 %copy-start.4 = (bf16[64,1024]{1,0:T(8,128)(2,1)S(1)}, bf16[64,1024]{1,0:T(8,128)(2,1)}, u32[]{:S(2)}) copy-start(bf16[64,1024]{1,0:T(8,128)(2,1)} %reshape.638) | copy-start | bytes 393220
  269.1 13.7 %copy-start.3 = (bf16[64,1024]{1,0:T(8,128)(2,1)S(1)}, bf16[64,1024]{1,0:T(8,128)(2,1)}, u32[]{:S(2)}) copy-start(bf16[64,1024]{1,0:T(8,128)(2,1)} %reshape.644) | copy-start | bytes 393220
  282.7 6.3 %copy-start.1 = (bf16[32,2,8,4096]{3,0,2,1:T(8,128)(2,1)S(1)}, bf16[32,2,8,4096]{3,0,2,1:T(8,128)(2,1)}, u32[]{:S(2)}) copy-start(bf16[32,2,8,4096]{3,0,2,1:T(8,128)(2,1)} %fusion.30) | copy-start | bytes 12582916
  293.5 108.0 %all-to-all-start.4 = ((bf16[32,2,8,4096]{3,2,1,0:T(8,128)(2,1)}), bf16[32,2,8,4096]{3,2,1,0:T(8,128)(2,1)}, u32[]{:S(2)}, u32[]{:S(2)}) async-start(bf16[32,2,8,4096]{3,2,1,0:T(8,128)(2,1)} %copy.239), calls=%async_computation.4 | async-start | bytes 8388608 | tf_op jit(solution)/shard_map/all_to_all | solution.py:143
  312.1 102.9 %copy-start.2 = (bf16[64,16,64]{2,0,1:T(8,128)(2,1)S(1)}, bf16[64,16,64]{2,0,1:T(8,128)(2,1)}, u32[]{:S(2)}) copy-start(bf16[64,16,64]{2,0,1:T(8,128)(2,1)} %get-tuple-element.38) | copy-start | bytes 393220
  312.1 103.9 %copy-start.7 = (f32[16,31]{1,0:T(8,128)S(1)}, f32[16,31]{1,0:T(8,128)}, u32[]{:S(2)}) copy-start(f32[16,31]{1,0:T(8,128)} %get-tuple-element.52) | copy-start | bytes 5956
  312.1 103.9 %copy-start.8 = (f32[16,31]{1,0:T(8,128)S(1)}, f32[16,31]{1,0:T(8,128)}, u32[]{:S(2)}) copy-start(f32[16,31]{1,0:T(8,128)} %get-tuple-element.53) | copy-start | bytes 5956
  312.1 103.9 %copy-start.9 = (f32[16,31]{1,0:T(8,128)S(1)}, f32[16,31]{1,0:T(8,128)}, u32[]{:S(2)}) copy-start(f32[16,31]{1,0:T(8,128)} %get-tuple-element.54) | copy-start | bytes 5956
  312.2 103.9 %copy-start.10 = (f32[16,31]{1,0:T(8,128)S(1)}, f32[16,31]{1,0:T(8,128)}, u32[]{:S(2)}) copy-start(f32[16,31]{1,0:T(8,128)} %get-tuple-element.55) | copy-start | bytes 5956
  312.2 103.9 %copy-start.11 = (f32[16,31]{1,0:T(8,128)S(1)}, f32[16,31]{1,0:T(8,128)}, u32[]{:S(2)}) copy-start(f32[16,31]{1,0:T(8,128)} %get-tuple-element.64) | copy-start | bytes 5956
  312.2 103.9 %copy-start.12 = (f32[16,31]{1,0:T(8,128)S(1)}, f32[16,31]{1,0:T(8,128)}, u32[]{:S(2)}) copy-start(f32[16,31]{1,0:T(8,128)} %get-tuple-element.69) | copy-start | bytes 5956
  401.5 110.0 %all-to-all-start.3 = ((bf16[32,2,8,4096]{3,2,1,0:T(8,128)(2,1)}), bf16[32,2,8,4096]{3,2,1,0:T(8,128)(2,1)}, u32[]{:S(2)}, u32[]{:S(2)}) async-start(bf16[32,2,8,4096]{3,2,1,0:T(8,128)(2,1)} %copy.232), calls=%async_computation.3 | async-start | bytes 8388608 | tf_op jit(solution)/shard_map/all_to_all | solution.py:143
  520.3 13.7 %copy-start.5 = (bf16[64,1024]{1,0:T(8,128)(2,1)S(1)}, bf16[64,1024]{1,0:T(8,128)(2,1)}, u32[]{:S(2)}) copy-start(bf16[64,1024]{1,0:T(8,128)(2,1)} %reshape.656) | copy-start | bytes 393220
  533.9 6.3 %copy-start = (bf16[16,64,32,128]{3,2,1,0:T(8,128)(2,1)S(1)}, bf16[16,64,32,128]{3,2,1,0:T(8,128)(2,1)}, u32[]{:S(2)}) copy-start(bf16[16,64,32,128]{3,2,1,0:T(8,128)(2,1)} %copy.236) | copy-start | bytes 25165828
  (1 other events, 0.5 us)

commit v3 on v2

--- a/solution.py
+++ b/solution.py
@@ -2,6 +2,7 @@
 import jax.numpy as jnp
 from jax import lax
 from jax.sharding import PartitionSpec as P
+from jax.experimental import pallas as pl
 
 CAP = 2
 SLAB_ROWS = 64
@@ -93,16 +94,58 @@
     return jnp.dot(tap_values, received.reshape(-1, width), preferred_element_type=jnp.float32)
 
 
-def visit_term(received, recv_off, shifts, weight, psf_index, coef_table, basis_x, basis_y):
+LANE = 128
+SPAN = 512
+
+
+def filter_mix_kernel(slab_ref, halo_ref, band_ref, mix_ref, acc_ref, out_ref):
+    full = jnp.concatenate([slab_ref[...], halo_ref[...]], axis=1)
+    bases = band_ref.shape[1] // LANE
+    for block in range(SPAN // LANE):
+        window = full[:, block * LANE : block * LANE + 2 * LANE]
+        filtered = jnp.dot(window, band_ref[...], preferred_element_type=jnp.float32)
+        filtered = filtered.astype(jnp.bfloat16)
+        stacked = jnp.concatenate(
+            [filtered[:, base * LANE : (base + 1) * LANE] for base in range(bases)], axis=0
+        )
+        term = jnp.dot(mix_ref[...], stacked, preferred_element_type=jnp.float32)
+        out_ref[:, block * LANE : (block + 1) * LANE] = (
+            acc_ref[:, block * LANE : (block + 1) * LANE] + term
+        )
+
+
+def filter_mix(slab_image, tap_values, mix_matrix, acc):
+    rows, width = slab_image.shape
+    bases, taps = tap_values.shape
+    padded = jnp.pad(slab_image, ((0, 0), (32, SPAN - 32)))
+    band_rows = jnp.pad(tap_values, ((0, 0), (15, 2 * LANE + 1 - 15 - taps)))
+    band = toeplitz(band_rows, LANE).transpose(2, 0, 1).reshape(2 * LANE, bases * LANE)
+    steps = width // SPAN
+    return pl.pallas_call(
+        filter_mix_kernel,
+        grid=(steps,),
+        in_specs=[
+            pl.BlockSpec((rows, SPAN), lambda k: (0, k)),
+            pl.BlockSpec((rows, LANE), lambda k: (0, (k + 1) * (SPAN // LANE))),
+            pl.BlockSpec((2 * LANE, bases * LANE), lambda k: (0, 0)),
+            pl.BlockSpec((rows, bases * rows), lambda k: (0, 0)),
+            pl.BlockSpec((rows, SPAN), lambda k: (0, k)),
+        ],
+        out_specs=pl.BlockSpec((rows, SPAN), lambda k: (0, k)),
+        out_shape=jax.ShapeDtypeStruct((rows, width), jnp.float32),
+        input_output_aliases={4: 0},
+    )(padded, padded, band, mix_matrix, acc)
+
+
+def visit_term(received, recv_off, shifts, weight, psf_index, coef_table, basis_x, basis_y, acc):
     warp_x = lanczos_taps(shifts[0])
     warp_y = lanczos_taps(shifts[1])
     slab_image = place(received, recv_off, warp_y).astype(jnp.bfloat16)
     tap_values = combined_taps(basis_x, warp_x).astype(jnp.bfloat16)
-    filtered = row_filter(slab_image, tap_values)
     class_hits = (psf_index == jnp.arange(coef_table.shape[0], dtype=jnp.int32)).astype(jnp.float32)
     coeffs = jnp.sum(class_hits[:, None] * coef_table, axis=0)
     mix_matrix = mixing(weight, coeffs, basis_y, SLAB_ROWS)
-    return jnp.dot(mix_matrix, filtered, preferred_element_type=jnp.float32)
+    return filter_mix(slab_image, tap_values, mix_matrix, acc)
 
 
 def shards(
@@ -135,8 +178,9 @@
             coef_table,
             basis_x,
             basis_y,
-        )
-        partial_sum = partial_sum + visit_part
+            partial_sum,
+        )
+        partial_sum = visit_part
         later = step_index + 2
         if later < step_count:
             released, partial_sum = lax.optimization_barrier((outgoing[later], partial_sum))

time: 588 us -> 543 us (0.923)
  Pallas kernels: 0 us -> 55.9 us
  local copies, waits for them, and re-layouts: 119 us -> 64.5 us
  matrix products: 73.1 us -> 22.2 us
  waiting for transfers between devices: 237 us -> 249 us
    pallas_call x0 -> x4, Pallas kernels: none -> 55.9 us  [filter_mix(): pl.pallas_call(filter_mix_kernel, grid=(steps,), in_specs=[pl.BlockSpec((...]
    convert_element_type x4 -> x0, local copies, waits for them, and re-layouts: 54.6 us -> none  [row_filter(): filtered.astype(jnp.bfloat16)]
    dot_general x8 -> x0, matrix products: 49.6 us -> none  [the longest x4 28.1 us: row_filter(): jnp.einsum('rna,boa->brno', windows, band_matrix, preferred_element_type=...]
    all_to_all x2, waiting for transfers between devices: 93.4 us -> 112 us  [shards(): lax.all_to_all(outgoing[step_index], 'patch', split_axis=0, concat_axis=0...]
    reshape x5 -> x1, local copies, waits for them, and re-layouts: 7.82 us -> 0.79 us  [toeplitz(): tiled[..., :count * length].reshape(period.shape[:-1] + (count, length))]
  transfers between devices with their start and end apart: 5 -> 5, of which waited for: 4 -> 4; matrix products, arithmetic and copies ran while one was open for 30% -> 23% of each run, Pallas kernels for 0% -> 5%
where the time goes in v3:
time: 543 us; the launch traced here: 535 us
  waiting for transfers between devices  249 us (46%)
  local copies, waits for them, and re-layouts  64.5 us (12%)
  starting transfers between devices  63.6 us (12%)
  Pallas kernels  55.9 us (10%)
  other arithmetic  46.8 us (9%)
  blocking collectives  31.8 us (6%)
  matrix products  22.2 us (4%)
    all_to_all x2, waiting for transfers between devices, shards(): lax.all_to_all(released, 'patch', split_axis=0, concat_axis=0, tiled=True)  137 us
    all_to_all x2, waiting for transfers between devices, shards(): lax.all_to_all(outgoing[step_index], 'patch', split_axis=0, concat_axis=0...  112 us
    pallas_call x4, Pallas kernels, filter_mix(): pl.pallas_call(filter_mix_kernel, grid=(steps,), in_specs=[pl.BlockSpec((...  55.9 us
    all_to_all x1, blocking collectives, shards(): lax.all_to_all(partial_sum.reshape(streams, share_rows, width), 'stream',...  31.8 us
    all_to_all x2, starting transfers between devices, shards(): lax.all_to_all(released, 'patch', split_axis=0, concat_axis=0, tiled=True)  26.9 us
    all_to_all x2, starting transfers between devices, shards(): lax.all_to_all(outgoing[step_index], 'patch', split_axis=0, concat_axis=0...  22.5 us
    mul x2, other arithmetic, combined_taps(): basis_rows * warp_x[tap_slot]  16.2 us
    all_to_all x1, starting transfers between devices, shards(): lax.all_to_all(slot_offsets, 'patch', split_axis=0, concat_axis=0, tiled=...  14.2 us
  transfers between devices with their start and end apart: 5, of which 4 were waited for; matrix products, arithmetic and copies ran while one was open for 23% of the time, Pallas kernels for 5%

profile of v3, /device:TPU:8, one launch (start us, length us, event | category | flops | bytes accessed | tf_op | source)
XLA Modules:
  0.0 535.4 jit_solution(2345929837349153635)
XLA Ops:
  6.0 14.2 %all-to-all-start = ((s32[32,4,2]{1,2,0:T(2,128)}), s32[32,4,2]{1,2,0:T(2,128)S(1)}, u32[]{:S(2)}, u32[]{:S(2)}) async-start(s32[32,4,2]{1,2,0:T(2,128)} %copy.123), calls=%async_computation | async-start | bytes 65536 | tf_op jit(solution)/shard_map/all_to_all | solution.py:163
  21.7 4.1 fusion.104
  27.3 4.2 copy.146
  31.6 12.2 %all-to-all-start.2 = ((bf16[32,2,8,4096]{3,2,1,0:T(8,128)(2,1)}), bf16[32,2,8,4096]{3,2,1,0:T(8,128)(2,1)}, u32[]{:S(2)}, u32[]{:S(2)}) async-start(bf16[32,2,8,4096]{3,2,1,0:T(8,128)(2,1)} %copy.146), calls=%async_computation.2 | async-start | bytes 8388608 | tf_op jit(solution)/shard_map/all_to_all | solution.py:167
  45.5 4.3 copy.134
  49.8 93.4 %all-to-all-done.2 = bf16[32,2,8,4096]{3,2,1,0:T(8,128)(2,1)} async-done(((bf16[32,2,8,4096]{3,2,1,0:T(8,128)(2,1)}), bf16[32,2,8,4096]{3,2,1,0:T(8,128)(2,1)}, u32[]{:S(2)}, u32[]{:S(2)}) %all-to-all-start.2) | async-done | bytes 4194336 | tf_op jit(solution)/shard_map/all_to_all | solution.py:167
  143.2 10.3 %all-to-all-start.1 = ((bf16[32,2,8,4096]{3,2,1,0:T(8,128)(2,1)}), bf16[32,2,8,4096]{3,2,1,0:T(8,128)(2,1)}, u32[]{:S(2)}, u32[]{:S(2)}) async-start(bf16[32,2,8,4096]{3,2,1,0:T(8,128)(2,1)} %copy.134), calls=%async_computation.1 | async-start | bytes 8388608 | tf_op jit(solution)/shard_map/all_to_all | solution.py:167
  167.1 4.3 broadcast_multiply_fusion.1
  171.5 11.8 %broadcast_multiply_fusion.5 = (f32[16,31]{1,0:T(8,128)S(1)}, f32[16,31]{1,0:T(8,128)S(1)}, f32[16,31]{1,0:T(8,128)S(1)}, f32[16,31]{1,0:T(8,128)S(1)}, f32[16,3...) fusion(f32[16,31]{1,0:T(8,128)S(1)} %copy-done.2, ...), kind=kLoop, calls=%fused_computation.103 | loop fusion | flops 8928 | bytes 37768 | tf_op jit(solution)/shard_map/mul | solution.py:20
  198.6 3.5 fusion.2
  205.2 3.1 convolution_convert_fusion.2
  210.4 14.1 %shard_map.91.acc_ref = f32[64,4096]{1,0:T(8,128)} custom-call(bf16[64,4608]{1,0:T(8,128)(2,1)} %pad.120.slab_ref.halo_ref, bf16[64,4608]{1,0:T(8,128)(2,1)} %pad.120.slab_ref.halo_ref, bf16[256,2048]{1,0:T(8,128)(2,1)} %copy.169.band_ref, bf16[64,1024]{1,0:T(8,128)(2,1)} %reshape.621.mix_ref, ...), custom_call_target="tpu_custom_call", output_to_operand_aliasing={{}: (4, {})} | custom-call | tf_op jit(solution)/shard_map/pallas_call | solution.py:124
  224.5 6.5 %copy.153 = bf16[32,2,8,4096]{3,2,1,0:T(8,128)(2,1)} copy(bf16[32,2,8,4096]{3,0,2,1:T(8,128)(2,1)} %fusion.2) | data formatting | bytes 8388608 | tf_op jit(solution)/shard_map/optimization_barrier | solution.py:186
  231.0 18.5 %all-to-all-done.1 = bf16[32,2,8,4096]{3,2,1,0:T(8,128)(2,1)} async-done(((bf16[32,2,8,4096]{3,2,1,0:T(8,128)(2,1)}), bf16[32,2,8,4096]{3,2,1,0:T(8,128)(2,1)}, u32[]{:S(2)}, u32[]{:S(2)}) %all-to-all-start.1) | async-done | bytes 4194336 | tf_op jit(solution)/shard_map/all_to_all | solution.py:167
  249.5 14.4 %all-to-all-start.4 = ((bf16[32,2,8,4096]{3,2,1,0:T(8,128)(2,1)}), bf16[32,2,8,4096]{3,2,1,0:T(8,128)(2,1)}, u32[]{:S(2)}, u32[]{:S(2)}) async-start(bf16[32,2,8,4096]{3,2,1,0:T(8,128)(2,1)} %copy.153), calls=%async_computation.4 | async-start | bytes 8388608 | tf_op jit(solution)/shard_map/all_to_all | solution.py:187
  271.4 3.5 fusion.6
  279.7 13.9 %shard_map.92.acc_ref = f32[64,4096]{1,0:T(8,128)} custom-call(bf16[64,4608]{1,0:T(8,128)(2,1)} %pad.111.slab_ref.halo_ref, bf16[64,4608]{1,0:T(8,128)(2,1)} %pad.111.slab_ref.halo_ref, bf16[256,2048]{1,0:T(8,128)(2,1)} %copy.164.band_ref, bf16[64,1024]{1,0:T(8,128)(2,1)} %reshape.617.mix_ref, ...), custom_call_target="tpu_custom_call", output_to_operand_aliasing={{}: (4, {})} | custom-call | tf_op jit(solution)/shard_map/pallas_call | solution.py:124
  293.6 6.4 %copy.149 = bf16[32,2,8,4096]{3,2,1,0:T(8,128)(2,1)} copy(bf16[32,2,8,4096]{3,0,2,1:T(8,128)(2,1)} %fusion.6) | data formatting | bytes 8388608 | tf_op jit(solution)/shard_map/optimization_barrier | solution.py:186
  300.1 61.0 %all-to-all-done.4 = bf16[32,2,8,4096]{3,2,1,0:T(8,128)(2,1)} async-done(((bf16[32,2,8,4096]{3,2,1,0:T(8,128)(2,1)}), bf16[32,2,8,4096]{3,2,1,0:T(8,128)(2,1)}, u32[]{:S(2)}, u32[]{:S(2)}) %all-to-all-start.4) | async-done | bytes 4194336 | tf_op jit(solution)/shard_map/all_to_all | solution.py:187
  361.1 12.5 %all-to-all-start.3 = ((bf16[32,2,8,4096]{3,2,1,0:T(8,128)(2,1)}), bf16[32,2,8,4096]{3,2,1,0:T(8,128)(2,1)}, u32[]{:S(2)}, u32[]{:S(2)}) async-start(bf16[32,2,8,4096]{3,2,1,0:T(8,128)(2,1)} %copy.149), calls=%async_computation.3 | async-start | bytes 8388608 | tf_op jit(solution)/shard_map/all_to_all | solution.py:187
  394.0 76.5 %all-to-all-done.3 = bf16[32,2,8,4096]{3,2,1,0:T(8,128)(2,1)} async-done(((bf16[32,2,8,4096]{3,2,1,0:T(8,128)(2,1)}), bf16[32,2,8,4096]{3,2,1,0:T(8,128)(2,1)}, u32[]{:S(2)}, u32[]{:S(2)}) %all-to-all-start.3) | async-done | bytes 4194336 | tf_op jit(solution)/shard_map/all_to_all | solution.py:187
  474.6 13.9 %shard_map.93.acc_ref = f32[64,4096]{1,0:T(8,128)} custom-call(bf16[64,4608]{1,0:T(8,128)(2,1)} %pad.136.slab_ref.halo_ref, bf16[64,4608]{1,0:T(8,128)(2,1)} %pad.136.slab_ref.halo_ref, bf16[256,2048]{1,0:T(8,128)(2,1)} %copy.171.band_ref, bf16[64,1024]{1,0:T(8,128)(2,1)} %reshape.629.mix_ref, ...), custom_call_target="tpu_custom_call", output_to_operand_aliasing={{}: (4, {})} | custom-call | tf_op jit(solution)/shard_map/pallas_call | solution.py:124
  488.5 13.9 %shard_map.94 = f32[64,4096]{1,0:T(8,128)} custom-call(bf16[64,4608]{1,0:T(8,128)(2,1)} %pad.128.slab_ref.halo_ref, bf16[64,4608]{1,0:T(8,128)(2,1)} %pad.128.slab_ref.halo_ref, bf16[256,2048]{1,0:T(8,128)(2,1)} %copy.170.band_ref, bf16[64,1024]{1,0:T(8,128)(2,1)} %reshape.625.mix_ref, f32[64,4096]{1,0:T(8,128)} %shard_map.93.acc_ref), custom_call_target="tpu_custom_call", output_to_operand_aliasing={{}: (4, {})} | custom-call | tf_op jit(solution)/shard_map/pallas_call | solution.py:124
  502.4 31.8 %all_to_all.30 = f32[8,8,4096]{2,1,0:T(8,128)S(1)} all-to-all(f32[8,8,4096]{2,1,0:T(8,128)} %bitcast.190), channel_id=1, replica_groups=mesh['patch'=32,'stream'=8] {'stream'}, dimensions={0} | all-to-all | bytes 2097152 | tf_op jit(solution)/shard_map/all_to_all | solution.py:191
  (205 shorter events, 82.0 us)
Async XLA Ops:
  6.0 25.6 %all-to-all-start = ((s32[32,4,2]{1,2,0:T(2,128)}), s32[32,4,2]{1,2,0:T(2,128)S(1)}, u32[]{:S(2)}, u32[]{:S(2)}) async-start(s32[32,4,2]{1,2,0:T(2,128)} %copy.123), calls=%async_computation | async-start | bytes 65536 | tf_op jit(solution)/shard_map/all_to_all | solution.py:163
  31.6 111.7 %all-to-all-start.2 = ((bf16[32,2,8,4096]{3,2,1,0:T(8,128)(2,1)}), bf16[32,2,8,4096]{3,2,1,0:T(8,128)(2,1)}, u32[]{:S(2)}, u32[]{:S(2)}) async-start(bf16[32,2,8,4096]{3,2,1,0:T(8,128)(2,1)} %copy.146), calls=%async_computation.2 | async-start | bytes 8388608 | tf_op jit(solution)/shard_map/all_to_all | solution.py:167
  49.8 103.7 %copy-start.9 = (f32[4,1,2]{0,2,1:T(2,128)S(1)}, f32[4,1,2]{0,2,1:T(2,128)}, u32[]{:S(2)}) copy-start(f32[4,1,2]{0,2,1:T(2,128)} %param.13) | copy-start | bytes 100
  49.8 117.3 %copy-start.2 = (f32[16,31]{1,0:T(8,128)S(1)}, f32[16,31]{1,0:T(8,128)}, u32[]{:S(2)}) copy-start(f32[16,31]{1,0:T(8,128)} %param.17) | copy-start | bytes 5956
  143.2 106.2 %all-to-all-start.1 = ((bf16[32,2,8,4096]{3,2,1,0:T(8,128)(2,1)}), bf16[32,2,8,4096]{3,2,1,0:T(8,128)(2,1)}, u32[]{:S(2)}, u32[]{:S(2)}) async-start(bf16[32,2,8,4096]{3,2,1,0:T(8,128)(2,1)} %copy.134), calls=%async_computation.1 | async-start | bytes 8388608 | tf_op jit(solution)/shard_map/all_to_all | solution.py:167
  183.6 3.7 copy-start.10
  185.5 2.9 copy-start.11
  185.5 6.0 %copy-start.12 = (f32[4,1]{0,1:T(1,128)S(1)}, f32[4,1]{0,1:T(1,128)}, u32[]{:S(2)}) copy-start(f32[4,1]{0,1:T(1,128)} %param.14) | copy-start | bytes 52
  185.5 6.6 %copy-start.13 = (f32[8,16]{1,0:T(8,128)S(1)}, f32[8,16]{1,0:T(8,128)}, u32[]{:S(2)}) copy-start(f32[8,16]{1,0:T(8,128)} %param.16) | copy-start | bytes 1540
  185.6 13.0 %copy-start.1 = (bf16[1,1,16,8,4096]{4,3,2,1,0:T(8,128)(2,1)S(1)}, bf16[1,1,16,8,4096]{4,3,2,1,0:T(8,128)(2,1)}, u32[]{:S(2)}) copy-start(bf16[1,1,16,8,4096]{4,3,2,1,0:T(8,128)(2,1)} %get-tuple-element.33) | copy-start | bytes 3145732
  249.5 111.6 %all-to-all-start.4 = ((bf16[32,2,8,4096]{3,2,1,0:T(8,128)(2,1)}), bf16[32,2,8,4096]{3,2,1,0:T(8,128)(2,1)}, u32[]{:S(2)}, u32[]{:S(2)}) async-start(bf16[32,2,8,4096]{3,2,1,0:T(8,128)(2,1)} %copy.153), calls=%async_computation.4 | async-start | bytes 8388608 | tf_op jit(solution)/shard_map/all_to_all | solution.py:187
  266.0 5.4 %copy-start = (bf16[1,1,16,8,4096]{4,3,2,1,0:T(8,128)(2,1)S(1)}, bf16[1,1,16,8,4096]{4,3,2,1,0:T(8,128)(2,1)}, u32[]{:S(2)}) copy-start(bf16[1,1,16,8,4096]{4,3,2,1,0:T(8,128)(2,1)} %get-tuple-element.32) | copy-start | bytes 3145732
  300.1 73.5 %copy-start.3 = (f32[16,31]{1,0:T(8,128)S(1)}, f32[16,31]{1,0:T(8,128)}, u32[]{:S(2)}) copy-start(f32[16,31]{1,0:T(8,128)} %get-tuple-element.44) | copy-start | bytes 5956
  300.1 73.5 %copy-start.4 = (f32[16,31]{1,0:T(8,128)S(1)}, f32[16,31]{1,0:T(8,128)}, u32[]{:S(2)}) copy-start(f32[16,31]{1,0:T(8,128)} %get-tuple-element.45) | copy-start | bytes 5956
  300.1 73.5 %copy-start.5 = (f32[16,31]{1,0:T(8,128)S(1)}, f32[16,31]{1,0:T(8,128)}, u32[]{:S(2)}) copy-start(f32[16,31]{1,0:T(8,128)} %get-tuple-element.46) | copy-start | bytes 5956
  300.1 73.5 %copy-start.6 = (f32[16,31]{1,0:T(8,128)S(1)}, f32[16,31]{1,0:T(8,128)}, u32[]{:S(2)}) copy-start(f32[16,31]{1,0:T(8,128)} %get-tuple-element.47) | copy-start | bytes 5956
  300.1 73.5 %copy-start.7 = (f32[16,31]{1,0:T(8,128)S(1)}, f32[16,31]{1,0:T(8,128)}, u32[]{:S(2)}) copy-start(f32[16,31]{1,0:T(8,128)} %get-tuple-element.56) | copy-start | bytes 5956
  300.1 73.5 %copy-start.8 = (f32[16,31]{1,0:T(8,128)S(1)}, f32[16,31]{1,0:T(8,128)}, u32[]{:S(2)}) copy-start(f32[16,31]{1,0:T(8,128)} %get-tuple-element.61) | copy-start | bytes 5956
  361.1 109.4 %all-to-all-start.3 = ((bf16[32,2,8,4096]{3,2,1,0:T(8,128)(2,1)}), bf16[32,2,8,4096]{3,2,1,0:T(8,128)(2,1)}, u32[]{:S(2)}, u32[]{:S(2)}) async-start(bf16[32,2,8,4096]{3,2,1,0:T(8,128)(2,1)} %copy.149), calls=%async_computation.3 | async-start | bytes 8388608 | tf_op jit(solution)/shard_map/all_to_all | solution.py:187

commit v4 on v3

--- a/solution.py
+++ b/solution.py
@@ -100,18 +100,28 @@
 
 def filter_mix_kernel(slab_ref, halo_ref, band_ref, mix_ref, acc_ref, out_ref):
     full = jnp.concatenate([slab_ref[...], halo_ref[...]], axis=1)
+    rows = slab_ref.shape[0]
+    blocks = SPAN // LANE
     bases = band_ref.shape[1] // LANE
-    for block in range(SPAN // LANE):
-        window = full[:, block * LANE : block * LANE + 2 * LANE]
-        filtered = jnp.dot(window, band_ref[...], preferred_element_type=jnp.float32)
-        filtered = filtered.astype(jnp.bfloat16)
-        stacked = jnp.concatenate(
-            [filtered[:, base * LANE : (base + 1) * LANE] for base in range(bases)], axis=0
-        )
-        term = jnp.dot(mix_ref[...], stacked, preferred_element_type=jnp.float32)
-        out_ref[:, block * LANE : (block + 1) * LANE] = (
-            acc_ref[:, block * LANE : (block + 1) * LANE] + term
-        )
+    windows = jnp.concatenate(
+        [full[:, block * LANE : block * LANE + 2 * LANE] for block in range(blocks)], axis=0
+    )
+    filtered = jnp.dot(windows, band_ref[...], preferred_element_type=jnp.float32)
+    filtered = filtered.astype(jnp.bfloat16)
+    stacked = jnp.concatenate(
+        [
+            jnp.concatenate(
+                [
+                    filtered[block * rows : (block + 1) * rows, base * LANE : (base + 1) * LANE]
+                    for block in range(blocks)
+                ],
+                axis=1,
+            )
+            for base in range(bases)
+        ],
+        axis=0,
+    )
+    out_ref[...] = acc_ref[...] + jnp.dot(mix_ref[...], stacked, preferred_element_type=jnp.float32)
 
 
 def filter_mix(slab_image, tap_values, mix_matrix, acc):
@@ -134,6 +144,11 @@
         out_specs=pl.BlockSpec((rows, SPAN), lambda k: (0, k)),
         out_shape=jax.ShapeDtypeStruct((rows, width), jnp.float32),
         input_output_aliases={4: 0},
+        cost_estimate=pl.CostEstimate(
+            flops=2 * rows * width * 2 * LANE * bases + 2 * rows * width * bases * rows,
+            transcendentals=0,
+            bytes_accessed=padded.size * 2 + band.size * 2 + mix_matrix.size * 2 + acc.size * 8,
+        ),
     )(padded, padded, band, mix_matrix, acc)
 
 

time: 543 us -> 533 us (0.982)
  Pallas kernels: 55.9 us -> 33.4 us
  waiting for transfers between devices: 249 us -> 259 us
    pallas_call x4, Pallas kernels: 55.9 us -> 33.4 us  [filter_mix(): pl.pallas_call(filter_mix_kernel, grid=(steps,), in_specs=[pl.BlockSpec((...]
    all_to_all x2, waiting for transfers between devices: 112 us -> 118 us  [shards(): lax.all_to_all(outgoing[step_index], 'patch', split_axis=0, concat_axis=0...]
  transfers between devices with their start and end apart: 5 -> 5, of which waited for: 4 -> 4; matrix products, arithmetic and copies ran while one was open for 23% -> 23% of each run, Pallas kernels for 5% -> 3%
where the time goes in v4:
time: 533 us; the launch traced here: 524 us
  waiting for transfers between devices  259 us (49%)
  local copies, waits for them, and re-layouts  64.5 us (12%)
  starting transfers between devices  64 us (12%)
  other arithmetic  46.8 us (9%)
  Pallas kernels  33.4 us (6%)
  blocking collectives  33.3 us (6%)
  matrix products  22.2 us (4%)
    all_to_all x2, waiting for transfers between devices, shards(): lax.all_to_all(released, 'patch', split_axis=0, concat_axis=0, tiled=True)  141 us
    all_to_all x2, waiting for transfers between devices, shards(): lax.all_to_all(outgoing[step_index], 'patch', split_axis=0, concat_axis=0...  118 us
    pallas_call x4, Pallas kernels, filter_mix(): pl.pallas_call(filter_mix_kernel, grid=(steps,), in_specs=[pl.BlockSpec((...  33.4 us
    all_to_all x1, blocking collectives, shards(): lax.all_to_all(partial_sum.reshape(streams, share_rows, width), 'stream',...  33.3 us
    all_to_all x2, starting transfers between devices, shards(): lax.all_to_all(released, 'patch', split_axis=0, concat_axis=0, tiled=True)  27.3 us
    all_to_all x2, starting transfers between devices, shards(): lax.all_to_all(outgoing[step_index], 'patch', split_axis=0, concat_axis=0...  22.5 us
    mul x2, other arithmetic, combined_taps(): basis_rows * warp_x[tap_slot]  16.2 us
    all_to_all x1, starting transfers between devices, shards(): lax.all_to_all(slot_offsets, 'patch', split_axis=0, concat_axis=0, tiled=...  14.2 us
  transfers between devices with their start and end apart: 5, of which 4 were waited for; matrix products, arithmetic and copies ran while one was open for 23% of the time, Pallas kernels for 3%

profile of v4, /device:TPU:8, one launch (start us, length us, event | category | flops | bytes accessed | tf_op | source)
XLA Modules:
  0.0 524.4 jit_solution(6582064570682381891)
XLA Ops:
  6.0 14.2 %all-to-all-start = ((s32[32,4,2]{1,2,0:T(2,128)}), s32[32,4,2]{1,2,0:T(2,128)S(1)}, u32[]{:S(2)}, u32[]{:S(2)}) async-start(s32[32,4,2]{1,2,0:T(2,128)} %copy.123), calls=%async_computation | async-start | bytes 65536 | tf_op jit(solution)/shard_map/all_to_all | solution.py:178
  21.7 4.1 fusion.104
  27.3 4.2 copy.146
  31.6 12.2 %all-to-all-start.2 = ((bf16[32,2,8,4096]{3,2,1,0:T(8,128)(2,1)}), bf16[32,2,8,4096]{3,2,1,0:T(8,128)(2,1)}, u32[]{:S(2)}, u32[]{:S(2)}) async-start(bf16[32,2,8,4096]{3,2,1,0:T(8,128)(2,1)} %copy.146), calls=%async_computation.2 | async-start | bytes 8388608 | tf_op jit(solution)/shard_map/all_to_all | solution.py:182
  45.5 4.3 copy.134
  49.8 93.4 %all-to-all-done.2 = bf16[32,2,8,4096]{3,2,1,0:T(8,128)(2,1)} async-done(((bf16[32,2,8,4096]{3,2,1,0:T(8,128)(2,1)}), bf16[32,2,8,4096]{3,2,1,0:T(8,128)(2,1)}, u32[]{:S(2)}, u32[]{:S(2)}) %all-to-all-start.2) | async-done | bytes 4194336 | tf_op jit(solution)/shard_map/all_to_all | solution.py:182
  143.2 10.3 %all-to-all-start.1 = ((bf16[32,2,8,4096]{3,2,1,0:T(8,128)(2,1)}), bf16[32,2,8,4096]{3,2,1,0:T(8,128)(2,1)}, u32[]{:S(2)}, u32[]{:S(2)}) async-start(bf16[32,2,8,4096]{3,2,1,0:T(8,128)(2,1)} %copy.134), calls=%async_computation.1 | async-start | bytes 8388608 | tf_op jit(solution)/shard_map/all_to_all | solution.py:182
  167.1 4.3 broadcast_multiply_fusion.1
  171.5 11.8 %broadcast_multiply_fusion.5 = (f32[16,31]{1,0:T(8,128)S(1)}, f32[16,31]{1,0:T(8,128)S(1)}, f32[16,31]{1,0:T(8,128)S(1)}, f32[16,31]{1,0:T(8,128)S(1)}, f32[16,3...) fusion(f32[16,31]{1,0:T(8,128)S(1)} %copy-done.2, ...), kind=kLoop, calls=%fused_computation.103 | loop fusion | flops 8928 | bytes 37768 | tf_op jit(solution)/shard_map/mul | solution.py:20
  198.6 3.5 fusion.2
  205.2 3.1 convolution_convert_fusion.2
  210.4 8.5 %shard_map.91.acc_ref = f32[64,4096]{1,0:T(8,128)} custom-call(bf16[64,4608]{1,0:T(8,128)(2,1)} %pad.120.slab_ref.halo_ref, bf16[64,4608]{1,0:T(8,128)(2,1)} %pad.120.slab_ref.halo_ref, bf16[256,2048]{1,0:T(8,128)(2,1)} %copy.169.band_ref, bf16[64,1024]{1,0:T(8,128)(2,1)} %reshape.621.mix_ref, ...), custom_call_target="tpu_custom_call", output_to_operand_aliasing={{}: (4, {})} | custom-call | flops 2684354560 | bytes 3866624 | tf_op jit(solution)/shard_map/pallas_call | solution.py:134
  218.9 6.5 %copy.153 = bf16[32,2,8,4096]{3,2,1,0:T(8,128)(2,1)} copy(bf16[32,2,8,4096]{3,0,2,1:T(8,128)(2,1)} %fusion.2) | data formatting | bytes 8388608 | tf_op jit(solution)/shard_map/optimization_barrier | solution.py:201
  225.4 24.1 %all-to-all-done.1 = bf16[32,2,8,4096]{3,2,1,0:T(8,128)(2,1)} async-done(((bf16[32,2,8,4096]{3,2,1,0:T(8,128)(2,1)}), bf16[32,2,8,4096]{3,2,1,0:T(8,128)(2,1)}, u32[]{:S(2)}, u32[]{:S(2)}) %all-to-all-start.1) | async-done | bytes 4194336 | tf_op jit(solution)/shard_map/all_to_all | solution.py:182
  249.5 14.4 %all-to-all-start.4 = ((bf16[32,2,8,4096]{3,2,1,0:T(8,128)(2,1)}), bf16[32,2,8,4096]{3,2,1,0:T(8,128)(2,1)}, u32[]{:S(2)}, u32[]{:S(2)}) async-start(bf16[32,2,8,4096]{3,2,1,0:T(8,128)(2,1)} %copy.153), calls=%async_computation.4 | async-start | bytes 8388608 | tf_op jit(solution)/shard_map/all_to_all | solution.py:202
  271.4 3.5 fusion.6
  279.7 8.3 %shard_map.92.acc_ref = f32[64,4096]{1,0:T(8,128)} custom-call(bf16[64,4608]{1,0:T(8,128)(2,1)} %pad.111.slab_ref.halo_ref, bf16[64,4608]{1,0:T(8,128)(2,1)} %pad.111.slab_ref.halo_ref, bf16[256,2048]{1,0:T(8,128)(2,1)} %copy.164.band_ref, bf16[64,1024]{1,0:T(8,128)(2,1)} %reshape.617.mix_ref, ...), custom_call_target="tpu_custom_call", output_to_operand_aliasing={{}: (4, {})} | custom-call | flops 2684354560 | bytes 3866624 | tf_op jit(solution)/shard_map/pallas_call | solution.py:134
  288.0 6.4 %copy.149 = bf16[32,2,8,4096]{3,2,1,0:T(8,128)(2,1)} copy(bf16[32,2,8,4096]{3,0,2,1:T(8,128)(2,1)} %fusion.6) | data formatting | bytes 8388608 | tf_op jit(solution)/shard_map/optimization_barrier | solution.py:201
  294.5 66.6 %all-to-all-done.4 = bf16[32,2,8,4096]{3,2,1,0:T(8,128)(2,1)} async-done(((bf16[32,2,8,4096]{3,2,1,0:T(8,128)(2,1)}), bf16[32,2,8,4096]{3,2,1,0:T(8,128)(2,1)}, u32[]{:S(2)}, u32[]{:S(2)}) %all-to-all-start.4) | async-done | bytes 4194336 | tf_op jit(solution)/shard_map/all_to_all | solution.py:202
  361.1 12.9 %all-to-all-start.3 = ((bf16[32,2,8,4096]{3,2,1,0:T(8,128)(2,1)}), bf16[32,2,8,4096]{3,2,1,0:T(8,128)(2,1)}, u32[]{:S(2)}, u32[]{:S(2)}) async-start(bf16[32,2,8,4096]{3,2,1,0:T(8,128)(2,1)} %copy.149), calls=%async_computation.3 | async-start | bytes 8388608 | tf_op jit(solution)/shard_map/all_to_all | solution.py:202
  394.4 74.8 %all-to-all-done.3 = bf16[32,2,8,4096]{3,2,1,0:T(8,128)(2,1)} async-done(((bf16[32,2,8,4096]{3,2,1,0:T(8,128)(2,1)}), bf16[32,2,8,4096]{3,2,1,0:T(8,128)(2,1)}, u32[]{:S(2)}, u32[]{:S(2)}) %all-to-all-start.3) | async-done | bytes 4194336 | tf_op jit(solution)/shard_map/all_to_all | solution.py:202
  473.3 8.3 %shard_map.93.acc_ref = f32[64,4096]{1,0:T(8,128)} custom-call(bf16[64,4608]{1,0:T(8,128)(2,1)} %pad.136.slab_ref.halo_ref, bf16[64,4608]{1,0:T(8,128)(2,1)} %pad.136.slab_ref.halo_ref, bf16[256,2048]{1,0:T(8,128)(2,1)} %copy.171.band_ref, bf16[64,1024]{1,0:T(8,128)(2,1)} %reshape.629.mix_ref, ...), custom_call_target="tpu_custom_call", output_to_operand_aliasing={{}: (4, {})} | custom-call | flops 2684354560 | bytes 3866624 | tf_op jit(solution)/shard_map/pallas_call | solution.py:134
  481.6 8.3 %shard_map.94 = f32[64,4096]{1,0:T(8,128)} custom-call(bf16[64,4608]{1,0:T(8,128)(2,1)} %pad.128.slab_ref.halo_ref, bf16[64,4608]{1,0:T(8,128)(2,1)} %pad.128.slab_ref.halo_ref, bf16[256,2048]{1,0:T(8,128)(2,1)} %copy.170.band_ref, bf16[64,1024]{1,0:T(8,128)(2,1)} %reshape.625.mix_ref, f32[64,4096]{1,0:T(8,128)} %shard_map.93.acc_ref), custom_call_target="tpu_custom_call", output_to_operand_aliasing={{}: (4, {})} | custom-call | flops 2684354560 | bytes 3866624 | tf_op jit(solution)/shard_map/pallas_call | solution.py:134
  489.9 33.3 %all_to_all.30 = f32[8,8,4096]{2,1,0:T(8,128)S(1)} all-to-all(f32[8,8,4096]{2,1,0:T(8,128)} %bitcast.190), channel_id=1, replica_groups=mesh['patch'=32,'stream'=8] {'stream'}, dimensions={0} | all-to-all | bytes 2097152 | tf_op jit(solution)/shard_map/all_to_all | solution.py:206
  (205 shorter events, 82.0 us)
Async XLA Ops:
  6.0 25.6 %all-to-all-start = ((s32[32,4,2]{1,2,0:T(2,128)}), s32[32,4,2]{1,2,0:T(2,128)S(1)}, u32[]{:S(2)}, u32[]{:S(2)}) async-start(s32[32,4,2]{1,2,0:T(2,128)} %copy.123), calls=%async_computation | async-start | bytes 65536 | tf_op jit(solution)/shard_map/all_to_all | solution.py:178
  31.6 111.7 %all-to-all-start.2 = ((bf16[32,2,8,4096]{3,2,1,0:T(8,128)(2,1)}), bf16[32,2,8,4096]{3,2,1,0:T(8,128)(2,1)}, u32[]{:S(2)}, u32[]{:S(2)}) async-start(bf16[32,2,8,4096]{3,2,1,0:T(8,128)(2,1)} %copy.146), calls=%async_computation.2 | async-start | bytes 8388608 | tf_op jit(solution)/shard_map/all_to_all | solution.py:182
  49.8 103.7 %copy-start.9 = (f32[4,1,2]{0,2,1:T(2,128)S(1)}, f32[4,1,2]{0,2,1:T(2,128)}, u32[]{:S(2)}) copy-start(f32[4,1,2]{0,2,1:T(2,128)} %param.13) | copy-start | bytes 100
  49.8 117.3 %copy-start.2 = (f32[16,31]{1,0:T(8,128)S(1)}, f32[16,31]{1,0:T(8,128)}, u32[]{:S(2)}) copy-start(f32[16,31]{1,0:T(8,128)} %param.17) | copy-start | bytes 5956
  143.2 106.2 %all-to-all-start.1 = ((bf16[32,2,8,4096]{3,2,1,0:T(8,128)(2,1)}), bf16[32,2,8,4096]{3,2,1,0:T(8,128)(2,1)}, u32[]{:S(2)}, u32[]{:S(2)}) async-start(bf16[32,2,8,4096]{3,2,1,0:T(8,128)(2,1)} %copy.134), calls=%async_computation.1 | async-start | bytes 8388608 | tf_op jit(solution)/shard_map/all_to_all | solution.py:182
  183.6 3.7 copy-start.10
  185.5 2.9 copy-start.11
  185.5 6.0 %copy-start.12 = (f32[4,1]{0,1:T(1,128)S(1)}, f32[4,1]{0,1:T(1,128)}, u32[]{:S(2)}) copy-start(f32[4,1]{0,1:T(1,128)} %param.14) | copy-start | bytes 52
  185.5 6.6 %copy-start.13 = (f32[8,16]{1,0:T(8,128)S(1)}, f32[8,16]{1,0:T(8,128)}, u32[]{:S(2)}) copy-start(f32[8,16]{1,0:T(8,128)} %param.16) | copy-start | bytes 1540
  185.6 13.0 %copy-start.1 = (bf16[1,1,16,8,4096]{4,3,2,1,0:T(8,128)(2,1)S(1)}, bf16[1,1,16,8,4096]{4,3,2,1,0:T(8,128)(2,1)}, u32[]{:S(2)}) copy-start(bf16[1,1,16,8,4096]{4,3,2,1,0:T(8,128)(2,1)} %get-tuple-element.33) | copy-start | bytes 3145732
  249.5 111.6 %all-to-all-start.4 = ((bf16[32,2,8,4096]{3,2,1,0:T(8,128)(2,1)}), bf16[32,2,8,4096]{3,2,1,0:T(8,128)(2,1)}, u32[]{:S(2)}, u32[]{:S(2)}) async-start(bf16[32,2,8,4096]{3,2,1,0:T(8,128)(2,1)} %copy.153), calls=%async_computation.4 | async-start | bytes 8388608 | tf_op jit(solution)/shard_map/all_to_all | solution.py:202
  266.0 5.4 %copy-start = (bf16[1,1,16,8,4096]{4,3,2,1,0:T(8,128)(2,1)S(1)}, bf16[1,1,16,8,4096]{4,3,2,1,0:T(8,128)(2,1)}, u32[]{:S(2)}) copy-start(bf16[1,1,16,8,4096]{4,3,2,1,0:T(8,128)(2,1)} %get-tuple-element.32) | copy-start | bytes 3145732
  294.4 79.6 %copy-start.3 = (f32[16,31]{1,0:T(8,128)S(1)}, f32[16,31]{1,0:T(8,128)}, u32[]{:S(2)}) copy-start(f32[16,31]{1,0:T(8,128)} %get-tuple-element.44) | copy-start | bytes 5956
  294.4 79.6 %copy-start.4 = (f32[16,31]{1,0:T(8,128)S(1)}, f32[16,31]{1,0:T(8,128)}, u32[]{:S(2)}) copy-start(f32[16,31]{1,0:T(8,128)} %get-tuple-element.45) | copy-start | bytes 5956
  294.4 79.6 %copy-start.5 = (f32[16,31]{1,0:T(8,128)S(1)}, f32[16,31]{1,0:T(8,128)}, u32[]{:S(2)}) copy-start(f32[16,31]{1,0:T(8,128)} %get-tuple-element.46) | copy-start | bytes 5956
  294.4 79.6 %copy-start.6 = (f32[16,31]{1,0:T(8,128)S(1)}, f32[16,31]{1,0:T(8,128)}, u32[]{:S(2)}) copy-start(f32[16,31]{1,0:T(8,128)} %get-tuple-element.47) | copy-start | bytes 5956
  294.5 79.6 %copy-start.7 = (f32[16,31]{1,0:T(8,128)S(1)}, f32[16,31]{1,0:T(8,128)}, u32[]{:S(2)}) copy-start(f32[16,31]{1,0:T(8,128)} %get-tuple-element.56) | copy-start | bytes 5956
  294.5 79.6 %copy-start.8 = (f32[16,31]{1,0:T(8,128)S(1)}, f32[16,31]{1,0:T(8,128)}, u32[]{:S(2)}) copy-start(f32[16,31]{1,0:T(8,128)} %get-tuple-element.61) | copy-start | bytes 5956
  361.1 108.2 %all-to-all-start.3 = ((bf16[32,2,8,4096]{3,2,1,0:T(8,128)(2,1)}), bf16[32,2,8,4096]{3,2,1,0:T(8,128)(2,1)}, u32[]{:S(2)}, u32[]{:S(2)}) async-start(bf16[32,2,8,4096]{3,2,1,0:T(8,128)(2,1)} %copy.149), calls=%async_computation.3 | async-start | bytes 8388608 | tf_op jit(solution)/shard_map/all_to_all | solution.py:202
